TPU v7x, 32 devices: a whole 2x2x4 slice. The times are simulated.
32 devices in a mesh: parts: 2 (over x), rows: 2 (over core), cols: 8 (over z, y).
Axes of the slice: x: 2, y: 2, z: 4, core: 2. Of those that a mesh axis runs over, the one named last changes fastest.
Arguments:
- src_feat: float32 [32, 131072], P(None, ('parts', 'rows', 'cols')), parts along dimension 1, may hold values from -0.75 to 0.75
- tgt_feat: float32 [32, 16384], P(None, ('parts', 'cols')), parts along dimension 1, may hold values from -0.75 to 0.75
- tgt_pot: float32 [16384], P(('parts', 'cols')), parts along dimension 0, may hold values from -25 to 25
- log_src: float32 [131072], P(('parts', 'rows', 'cols')), parts along dimension 0, may hold values from -3 to 3
- log_tgt: float32 [16384], P(('parts', 'cols')), parts along dimension 0, may hold values from -3 to 3
- pairs: int32 [512, 24], P(('parts', 'rows', 'cols')), parts along dimension 0, may hold values from 0 to 31, as said below
- counts: int32 [512], P(('parts', 'rows', 'cols')), parts along dimension 0, may hold values from 1 to 24, as said below
Outputs:
- src_pot: float32 [131072], P(('parts', 'rows', 'cols')), parts along dimension 0
- new_tgt_pot: float32 [16384], P(('parts', 'cols')), parts along dimension 0
There are 2 independent parts, one for each index of `parts`. A program takes and returns all parts, laid end to end along the dimension named above; each array names one. Nothing has to cross between parts.
Inputs may be any that keep to these rules, and one draw needn't show every extreme that they name: `pairs`: each row names 24 different target blocks, and every target block is the first entry of some row. `counts`: row 0 uses all 24 entries and row 1 only one.
All inputs are finite; a program needn't handle non-finite values.
Results may differ from a plain program's by a relative error of at most 0.0003.
Values sent between devices are 32-bit elements; how exact they have to be, the bound alone decides.
No kernel may reach another device: no remote copies, remote signals or barrier semaphores. Data moves between devices by JAX's collectives and lax.ppermute only.
A program may use at most 128 MiB of HBM per device.

v0:
```python
import jax
import jax.numpy as jnp
from jax import lax
from jax.sharding import PartitionSpec as P

D = 32
BLK = 256
GROUP = 8


epsilon = 0.1
NEG = -1e30


def joined(array, axis, combine):
    everything = jax.tree.map(lambda part: lax.all_gather(part, axis), array)
    initial = jax.tree.map(lambda part: part[0], everything)

    def step(k, so_far):
        return combine(so_far, jax.tree.map(lambda part: part[k], everything))

    return lax.fori_loop(1, lax.axis_size(axis), step, initial)


def combine_parts(first, second):
    top = jnp.maximum(first[0], second[0])
    total = first[1] * jnp.exp(first[0] - top) + second[1] * jnp.exp(second[0] - top)
    return (top, total)


def on_device(src_feat, tgt_feat, tgt_pot, log_src, log_tgt, pairs, counts):
    own_targets = tgt_feat.shape[1]
    packed = jnp.concatenate([tgt_feat, tgt_pot[None, :], log_tgt[None, :]], axis=0)
    whole = lax.all_gather(packed, "cols", axis=1, tiled=True)
    feats = whole[:D]
    ynorm = jnp.sum(feats * feats, axis=0)
    tblocks = whole.shape[1] // BLK
    table = jnp.concatenate([whole, ynorm[None, :]], axis=0)
    blocks = jnp.transpose(table.reshape(D + 3, tblocks, BLK), (1, 0, 2))
    within = jnp.arange(GROUP, dtype=jnp.int32)
    block_numbers = jnp.arange(tblocks, dtype=jnp.int32)

    def row_step(carry, index):
        start = index * BLK
        xs = lax.dynamic_slice_in_dim(src_feat, start, BLK, 1)
        weights = lax.dynamic_slice_in_dim(log_src, start, BLK, 0)
        xnorm = jnp.sum(xs * xs, axis=0)
        row_ids = pairs[index]
        count = counts[index]
        ngroups = (count + GROUP - 1) // GROUP
        slabs = jnp.take(blocks, row_ids, axis=0)

        def take_group(step):
            ids = lax.dynamic_slice_in_dim(row_ids, step * GROUP, GROUP, 0)
            group = lax.dynamic_slice_in_dim(slabs, step * GROUP, GROUP, 0)
            mask = jnp.repeat(step * GROUP + within < count, BLK)
            cross = jnp.einsum(
                "dr,gdc->rgc",
                xs,
                group[:, :D, :],
                precision=lax.Precision.HIGHEST,
                preferred_element_type=jnp.float32,
            ).reshape(BLK, GROUP * BLK)
            cost = xnorm[:, None] + group[:, D + 2, :].reshape(-1)[None, :] - 2.0 * cross
            return (ids, mask, group, cost)

        def row_pass(step, state):
            run_top, run_sum = state
            ids, mask, group, cost = take_group(step)
            pots = group[:, D, :].reshape(-1)
            logs = group[:, D + 1, :].reshape(-1)
            scores = jnp.where(mask[None, :], logs[None, :] + (pots[None, :] - cost) / epsilon, NEG)
            top = jnp.maximum(run_top, jnp.max(scores, axis=1))
            run_sum = run_sum * jnp.exp(run_top - top) + jnp.sum(
                jnp.exp(scores - top[:, None]), axis=1
            )
            return (top, run_sum)

        start_state = (jnp.full((BLK,), NEG, jnp.float32), jnp.zeros((BLK,), jnp.float32))
        run_top, run_sum = lax.fori_loop(0, ngroups, row_pass, start_state)
        fpot = -epsilon * (run_top + jnp.log(run_sum))

        def col_pass(step, state):
            acc_top, acc_sum = state
            ids, mask, group, cost = take_group(step)
            scores = jnp.where(
                mask[None, :], weights[:, None] + (fpot[:, None] - cost) / epsilon, NEG
            )
            col_top = jnp.max(scores, axis=0)
            col_sum = jnp.where(mask, jnp.sum(jnp.exp(scores - col_top[None, :]), axis=0), 0.0)
            col_top = col_top.reshape(GROUP, BLK)
            col_sum = col_sum.reshape(GROUP, BLK)
            selector = ids[:, None] == block_numbers[None, :]
            onehot = selector.astype(jnp.float32)
            landed = jnp.max(jnp.where(selector[:, :, None], col_top[:, None, :], NEG), axis=0)
            top = jnp.maximum(acc_top, landed)
            top_here = jnp.einsum(
                "gt,tb->gb",
                onehot,
                top,
                precision=lax.Precision.HIGHEST,
                preferred_element_type=jnp.float32,
            )
            added = jnp.einsum(
                "gt,gb->tb",
                onehot,
                col_sum * jnp.exp(col_top - top_here),
                precision=lax.Precision.HIGHEST,
                preferred_element_type=jnp.float32,
            )
            fresh = acc_sum * jnp.exp(acc_top - top) + added
            return (top, fresh)

        carry = lax.fori_loop(0, ngroups, col_pass, carry)
        return (carry, fpot)

    init = (jnp.full((tblocks, BLK), NEG, jnp.float32), jnp.zeros((tblocks, BLK), jnp.float32))
    (acc_top, acc_sum), fblocks = lax.scan(
        row_step, init, jnp.arange(pairs.shape[0], dtype=jnp.int32)
    )
    src_pot = fblocks.reshape(-1)
    flat_top = acc_top.reshape(-1)
    flat_sum = acc_sum.reshape(-1)
    owner_start = lax.axis_index("cols") * own_targets
    all_top, all_sum = joined((flat_top, flat_sum), ("rows", "cols"), combine_parts)
    own_top = lax.dynamic_slice_in_dim(all_top, owner_start, own_targets, 0)
    own_sum = lax.dynamic_slice_in_dim(all_sum, owner_start, own_targets, 0)
    new_tgt_pot = -epsilon * (own_top + jnp.log(own_sum))
    return (src_pot, new_tgt_pot)


def solution(mesh):
    placed = (
        P(None, ("parts", "rows", "cols")),
        P(None, ("parts", "cols")),
        P(("parts", "cols")),
        P(("parts", "rows", "cols")),
        P(("parts", "cols")),
        P(("parts", "rows", "cols"), None),
        P(("parts", "rows", "cols")),
    )
    return jax.shard_map(
        on_device,
        mesh=mesh,
        in_specs=placed,
        out_specs=(P(("parts", "rows", "cols")), P(("parts", "cols"))),
        check_vma=False,
    )
```

profile of v0, /device:TPU:0, one launch (start us, length us, event | category | flops | bytes accessed | tf_op | source)
XLA Modules:
  0.0 660.5 jit_solution(5542897578245292571)
XLA Ops:
  8.9 46.1 %all-gather.4.cloned.1.call-done = f32[34,8192]{1,0:T(8,128)} async-done(((f32[34,1024]{1,0:T(8,128)}), f32[34,8192]{1,0:T(8,128)}) %all-gather.4.cloned.1.call-update) | async-done | bytes 1114128 | tf_op jit(solution)/shard_map/all_gather | solution.py:34
  57.9 512.1 %while.113 = (s32[]{:T(128)}, f32[32,256]{1,0:T(8,128)S(1)}, f32[32,256]{1,0:T(8,128)S(1)}, f32[16,256]{1,0:T(8,128)S(1)}, s32[16]{0:T(128)S(1)}, /*index=5*/s32...) while((s32[]{:T(128)}, f32[32,256]{1,0:T(8,128)S(1)}, ...), condition=%wide.region_12.13_spmd.clone.clone, body=%wide.region_1.12_spmd.clone.clone.sunk | while | flops 415103776 | bytes 13110493 | solution.py:118
  65.5 12.1 %while.114 = (s32[]{:T(128)}, f32[256]{0:T(256)S(1)}, f32[256]{0:T(256)S(1)}, s32[]{:T(128)}, s32[8]{0:T(128)S(1)}, /*index=5*/s32[]{:T(128)}, f32[24,35,256]{2,...) while((s32[]{:T(128)}, f32[256]{0:T(256)S(1)}, ...), condition=%wide.region_6.6_spmd, body=%wide.region_3.5_spmd.sunk | while | flops 206570016 | bytes 4627243 | solution.py:80
  66.3 2.9 fusion.43
  70.3 2.9 fusion.43
  74.4 2.9 fusion.43
  78.4 12.5 %while.115 = (s32[]{:T(128)}, f32[32,256]{1,0:T(8,128)S(1)}, f32[32,256]{1,0:T(8,128)S(1)}, s32[]{:T(128)}, s32[24]{0:T(128)S(1)}, /*index=5*/s32[32]{0:T(128)S(...) while((s32[]{:T(128)}, f32[32,256]{1,0:T(8,128)S(1)}, ...), condition=%wide.region_11.11_spmd, body=%wide.region_7.10_spmd.sunk | while | flops 208300816 | bytes 4961095 | solution.py:114
  98.5 4.1 while.114
  99.3 2.9 fusion.43
  103.4 4.1 while.115
  115.1 12.1 %while.114 = (s32[]{:T(128)}, f32[256]{0:T(256)S(1)}, f32[256]{0:T(256)S(1)}, s32[]{:T(128)}, s32[8]{0:T(128)S(1)}, /*index=5*/s32[]{:T(128)}, f32[24,35,256]{2,...) while((s32[]{:T(128)}, f32[256]{0:T(256)S(1)}, ...), condition=%wide.region_6.6_spmd, body=%wide.region_3.5_spmd.sunk | while | flops 206570016 | bytes 4627243 | solution.py:80
  115.9 2.9 fusion.43
  119.9 2.9 fusion.43
  124.0 2.9 fusion.43
  128.0 12.5 %while.115 = (s32[]{:T(128)}, f32[32,256]{1,0:T(8,128)S(1)}, f32[32,256]{1,0:T(8,128)S(1)}, s32[]{:T(128)}, s32[24]{0:T(128)S(1)}, /*index=5*/s32[32]{0:T(128)S(...) while((s32[]{:T(128)}, f32[32,256]{1,0:T(8,128)S(1)}, ...), condition=%wide.region_11.11_spmd, body=%wide.region_7.10_spmd.sunk | while | flops 208300816 | bytes 4961095 | solution.py:114
  148.1 12.1 %while.114 = (s32[]{:T(128)}, f32[256]{0:T(256)S(1)}, f32[256]{0:T(256)S(1)}, s32[]{:T(128)}, s32[8]{0:T(128)S(1)}, /*index=5*/s32[]{:T(128)}, f32[24,35,256]{2,...) while((s32[]{:T(128)}, f32[256]{0:T(256)S(1)}, ...), condition=%wide.region_6.6_spmd, body=%wide.region_3.5_spmd.sunk | while | flops 206570016 | bytes 4627243 | solution.py:80
  148.9 2.9 fusion.43
  157.0 2.9 fusion.43
  161.1 12.5 %while.115 = (s32[]{:T(128)}, f32[32,256]{1,0:T(8,128)S(1)}, f32[32,256]{1,0:T(8,128)S(1)}, s32[]{:T(128)}, s32[24]{0:T(128)S(1)}, /*index=5*/s32[32]{0:T(128)S(...) while((s32[]{:T(128)}, f32[32,256]{1,0:T(8,128)S(1)}, ...), condition=%wide.region_11.11_spmd, body=%wide.region_7.10_spmd.sunk | while | flops 208300816 | bytes 4961095 | solution.py:114
  181.2 12.1 %while.114 = (s32[]{:T(128)}, f32[256]{0:T(256)S(1)}, f32[256]{0:T(256)S(1)}, s32[]{:T(128)}, s32[8]{0:T(128)S(1)}, /*index=5*/s32[]{:T(128)}, f32[24,35,256]{2,...) while((s32[]{:T(128)}, f32[256]{0:T(256)S(1)}, ...), condition=%wide.region_6.6_spmd, body=%wide.region_3.5_spmd.sunk | while | flops 206570016 | bytes 4627243 | solution.py:80
  182.0 2.9 fusion.43
  190.1 2.9 fusion.43
  194.1 12.5 %while.115 = (s32[]{:T(128)}, f32[32,256]{1,0:T(8,128)S(1)}, f32[32,256]{1,0:T(8,128)S(1)}, s32[]{:T(128)}, s32[24]{0:T(128)S(1)}, /*index=5*/s32[32]{0:T(128)S(...) while((s32[]{:T(128)}, f32[32,256]{1,0:T(8,128)S(1)}, ...), condition=%wide.region_11.11_spmd, body=%wide.region_7.10_spmd.sunk | while | flops 208300816 | bytes 4961095 | solution.py:114
  214.2 12.1 %while.114 = (s32[]{:T(128)}, f32[256]{0:T(256)S(1)}, f32[256]{0:T(256)S(1)}, s32[]{:T(128)}, s32[8]{0:T(128)S(1)}, /*index=5*/s32[]{:T(128)}, f32[24,35,256]{2,...) while((s32[]{:T(128)}, f32[256]{0:T(256)S(1)}, ...), condition=%wide.region_6.6_spmd, body=%wide.region_3.5_spmd.sunk | while | flops 206570016 | bytes 4627243 | solution.py:80
  215.0 2.9 fusion.43
  223.1 2.9 fusion.43
  227.2 12.5 %while.115 = (s32[]{:T(128)}, f32[32,256]{1,0:T(8,128)S(1)}, f32[32,256]{1,0:T(8,128)S(1)}, s32[]{:T(128)}, s32[24]{0:T(128)S(1)}, /*index=5*/s32[32]{0:T(128)S(...) while((s32[]{:T(128)}, f32[32,256]{1,0:T(8,128)S(1)}, ...), condition=%wide.region_11.11_spmd, body=%wide.region_7.10_spmd.sunk | while | flops 208300816 | bytes 4961095 | solution.py:114
  247.2 12.1 %while.114 = (s32[]{:T(128)}, f32[256]{0:T(256)S(1)}, f32[256]{0:T(256)S(1)}, s32[]{:T(128)}, s32[8]{0:T(128)S(1)}, /*index=5*/s32[]{:T(128)}, f32[24,35,256]{2,...) while((s32[]{:T(128)}, f32[256]{0:T(256)S(1)}, ...), condition=%wide.region_6.6_spmd, body=%wide.region_3.5_spmd.sunk | while | flops 206570016 | bytes 4627243 | solution.py:80
  248.0 2.9 fusion.43
  256.1 2.9 fusion.43
  260.2 12.5 %while.115 = (s32[]{:T(128)}, f32[32,256]{1,0:T(8,128)S(1)}, f32[32,256]{1,0:T(8,128)S(1)}, s32[]{:T(128)}, s32[24]{0:T(128)S(1)}, /*index=5*/s32[32]{0:T(128)S(...) while((s32[]{:T(128)}, f32[32,256]{1,0:T(8,128)S(1)}, ...), condition=%wide.region_11.11_spmd, body=%wide.region_7.10_spmd.sunk | while | flops 208300816 | bytes 4961095 | solution.py:114
  280.3 12.1 %while.114 = (s32[]{:T(128)}, f32[256]{0:T(256)S(1)}, f32[256]{0:T(256)S(1)}, s32[]{:T(128)}, s32[8]{0:T(128)S(1)}, /*index=5*/s32[]{:T(128)}, f32[24,35,256]{2,...) while((s32[]{:T(128)}, f32[256]{0:T(256)S(1)}, ...), condition=%wide.region_6.6_spmd, body=%wide.region_3.5_spmd.sunk | while | flops 206570016 | bytes 4627243 | solution.py:80
  281.1 2.9 fusion.43
  293.2 12.5 %while.115 = (s32[]{:T(128)}, f32[32,256]{1,0:T(8,128)S(1)}, f32[32,256]{1,0:T(8,128)S(1)}, s32[]{:T(128)}, s32[24]{0:T(128)S(1)}, /*index=5*/s32[32]{0:T(128)S(...) while((s32[]{:T(128)}, f32[32,256]{1,0:T(8,128)S(1)}, ...), condition=%wide.region_11.11_spmd, body=%wide.region_7.10_spmd.sunk | while | flops 208300816 | bytes 4961095 | solution.py:114
  313.3 12.1 %while.114 = (s32[]{:T(128)}, f32[256]{0:T(256)S(1)}, f32[256]{0:T(256)S(1)}, s32[]{:T(128)}, s32[8]{0:T(128)S(1)}, /*index=5*/s32[]{:T(128)}, f32[24,35,256]{2,...) while((s32[]{:T(128)}, f32[256]{0:T(256)S(1)}, ...), condition=%wide.region_6.6_spmd, body=%wide.region_3.5_spmd.sunk | while | flops 206570016 | bytes 4627243 | solution.py:80
  314.1 2.9 fusion.43
  322.2 2.9 fusion.43
  326.3 12.5 %while.115 = (s32[]{:T(128)}, f32[32,256]{1,0:T(8,128)S(1)}, f32[32,256]{1,0:T(8,128)S(1)}, s32[]{:T(128)}, s32[24]{0:T(128)S(1)}, /*index=5*/s32[32]{0:T(128)S(...) while((s32[]{:T(128)}, f32[32,256]{1,0:T(8,128)S(1)}, ...), condition=%wide.region_11.11_spmd, body=%wide.region_7.10_spmd.sunk | while | flops 208300816 | bytes 4961095 | solution.py:114
  346.4 12.1 %while.114 = (s32[]{:T(128)}, f32[256]{0:T(256)S(1)}, f32[256]{0:T(256)S(1)}, s32[]{:T(128)}, s32[8]{0:T(128)S(1)}, /*index=5*/s32[]{:T(128)}, f32[24,35,256]{2,...) while((s32[]{:T(128)}, f32[256]{0:T(256)S(1)}, ...), condition=%wide.region_6.6_spmd, body=%wide.region_3.5_spmd.sunk | while | flops 206570016 | bytes 4627243 | solution.py:80
  359.3 12.5 %while.115 = (s32[]{:T(128)}, f32[32,256]{1,0:T(8,128)S(1)}, f32[32,256]{1,0:T(8,128)S(1)}, s32[]{:T(128)}, s32[24]{0:T(128)S(1)}, /*index=5*/s32[32]{0:T(128)S(...) while((s32[]{:T(128)}, f32[32,256]{1,0:T(8,128)S(1)}, ...), condition=%wide.region_11.11_spmd, body=%wide.region_7.10_spmd.sunk | while | flops 208300816 | bytes 4961095 | solution.py:114
  379.4 12.1 %while.114 = (s32[]{:T(128)}, f32[256]{0:T(256)S(1)}, f32[256]{0:T(256)S(1)}, s32[]{:T(128)}, s32[8]{0:T(128)S(1)}, /*index=5*/s32[]{:T(128)}, f32[24,35,256]{2,...) while((s32[]{:T(128)}, f32[256]{0:T(256)S(1)}, ...), condition=%wide.region_6.6_spmd, body=%wide.region_3.5_spmd.sunk | while | flops 206570016 | bytes 4627243 | solution.py:80
  380.2 2.9 fusion.43
  388.3 2.9 fusion.43
  392.3 12.5 %while.115 = (s32[]{:T(128)}, f32[32,256]{1,0:T(8,128)S(1)}, f32[32,256]{1,0:T(8,128)S(1)}, s32[]{:T(128)}, s32[24]{0:T(128)S(1)}, /*index=5*/s32[32]{0:T(128)S(...) while((s32[]{:T(128)}, f32[32,256]{1,0:T(8,128)S(1)}, ...), condition=%wide.region_11.11_spmd, body=%wide.region_7.10_spmd.sunk | while | flops 208300816 | bytes 4961095 | solution.py:114
  412.4 12.1 %while.114 = (s32[]{:T(128)}, f32[256]{0:T(256)S(1)}, f32[256]{0:T(256)S(1)}, s32[]{:T(128)}, s32[8]{0:T(128)S(1)}, /*index=5*/s32[]{:T(128)}, f32[24,35,256]{2,...) while((s32[]{:T(128)}, f32[256]{0:T(256)S(1)}, ...), condition=%wide.region_6.6_spmd, body=%wide.region_3.5_spmd.sunk | while | flops 206570016 | bytes 4627243 | solution.py:80
  421.3 2.9 fusion.43
  425.4 12.5 %while.115 = (s32[]{:T(128)}, f32[32,256]{1,0:T(8,128)S(1)}, f32[32,256]{1,0:T(8,128)S(1)}, s32[]{:T(128)}, s32[24]{0:T(128)S(1)}, /*index=5*/s32[32]{0:T(128)S(...) while((s32[]{:T(128)}, f32[32,256]{1,0:T(8,128)S(1)}, ...), condition=%wide.region_11.11_spmd, body=%wide.region_7.10_spmd.sunk | while | flops 208300816 | bytes 4961095 | solution.py:114
  445.5 12.1 %while.114 = (s32[]{:T(128)}, f32[256]{0:T(256)S(1)}, f32[256]{0:T(256)S(1)}, s32[]{:T(128)}, s32[8]{0:T(128)S(1)}, /*index=5*/s32[]{:T(128)}, f32[24,35,256]{2,...) while((s32[]{:T(128)}, f32[256]{0:T(256)S(1)}, ...), condition=%wide.region_6.6_spmd, body=%wide.region_3.5_spmd.sunk | while | flops 206570016 | bytes 4627243 | solution.py:80
  446.2 2.9 fusion.43
  454.3 2.9 fusion.43
  458.4 12.5 %while.115 = (s32[]{:T(128)}, f32[32,256]{1,0:T(8,128)S(1)}, f32[32,256]{1,0:T(8,128)S(1)}, s32[]{:T(128)}, s32[24]{0:T(128)S(1)}, /*index=5*/s32[32]{0:T(128)S(...) while((s32[]{:T(128)}, f32[32,256]{1,0:T(8,128)S(1)}, ...), condition=%wide.region_11.11_spmd, body=%wide.region_7.10_spmd.sunk | while | flops 208300816 | bytes 4961095 | solution.py:114
  478.5 12.1 %while.114 = (s32[]{:T(128)}, f32[256]{0:T(256)S(1)}, f32[256]{0:T(256)S(1)}, s32[]{:T(128)}, s32[8]{0:T(128)S(1)}, /*index=5*/s32[]{:T(128)}, f32[24,35,256]{2,...) while((s32[]{:T(128)}, f32[256]{0:T(256)S(1)}, ...), condition=%wide.region_6.6_spmd, body=%wide.region_3.5_spmd.sunk | while | flops 206570016 | bytes 4627243 | solution.py:80
  487.4 2.9 fusion.43
  491.4 12.5 %while.115 = (s32[]{:T(128)}, f32[32,256]{1,0:T(8,128)S(1)}, f32[32,256]{1,0:T(8,128)S(1)}, s32[]{:T(128)}, s32[24]{0:T(128)S(1)}, /*index=5*/s32[32]{0:T(128)S(...) while((s32[]{:T(128)}, f32[32,256]{1,0:T(8,128)S(1)}, ...), condition=%wide.region_11.11_spmd, body=%wide.region_7.10_spmd.sunk | while | flops 208300816 | bytes 4961095 | solution.py:114
  511.5 12.1 %while.114 = (s32[]{:T(128)}, f32[256]{0:T(256)S(1)}, f32[256]{0:T(256)S(1)}, s32[]{:T(128)}, s32[8]{0:T(128)S(1)}, /*index=5*/s32[]{:T(128)}, f32[24,35,256]{2,...) while((s32[]{:T(128)}, f32[256]{0:T(256)S(1)}, ...), condition=%wide.region_6.6_spmd, body=%wide.region_3.5_spmd.sunk | while | flops 206570016 | bytes 4627243 | solution.py:80
  512.3 2.9 fusion.43
  520.4 2.9 fusion.43
  524.5 12.5 %while.115 = (s32[]{:T(128)}, f32[32,256]{1,0:T(8,128)S(1)}, f32[32,256]{1,0:T(8,128)S(1)}, s32[]{:T(128)}, s32[24]{0:T(128)S(1)}, /*index=5*/s32[32]{0:T(128)S(...) while((s32[]{:T(128)}, f32[32,256]{1,0:T(8,128)S(1)}, ...), condition=%wide.region_11.11_spmd, body=%wide.region_7.10_spmd.sunk | while | flops 208300816 | bytes 4961095 | solution.py:114
  544.6 12.1 %while.114 = (s32[]{:T(128)}, f32[256]{0:T(256)S(1)}, f32[256]{0:T(256)S(1)}, s32[]{:T(128)}, s32[8]{0:T(128)S(1)}, /*index=5*/s32[]{:T(128)}, f32[24,35,256]{2,...) while((s32[]{:T(128)}, f32[256]{0:T(256)S(1)}, ...), condition=%wide.region_6.6_spmd, body=%wide.region_3.5_spmd.sunk | while | flops 206570016 | bytes 4627243 | solution.py:80
  545.4 2.9 fusion.43
  553.5 2.9 fusion.43
  557.5 12.5 %while.115 = (s32[]{:T(128)}, f32[32,256]{1,0:T(8,128)S(1)}, f32[32,256]{1,0:T(8,128)S(1)}, s32[]{:T(128)}, s32[24]{0:T(128)S(1)}, /*index=5*/s32[32]{0:T(128)S(...) while((s32[]{:T(128)}, f32[32,256]{1,0:T(8,128)S(1)}, ...), condition=%wide.region_11.11_spmd, body=%wide.region_7.10_spmd.sunk | while | flops 208300816 | bytes 4961095 | solution.py:114
  570.1 48.5 %all-gather.1 = f32[16,1,8192]{2,1,0:T(1,128)S(1)} all-gather(f32[1,1,8192]{2,1,0:T(1,128)S(1)} %reshape.237), channel_id=1, replica_groups=mesh['parts'=2,'rows'=2,'cols'=8] {'rows','cols'}, dimensions={0}, use_global_device_ids=true | all-gather | bytes 557056 | tf_op jit(solution)/shard_map/all_gather | solution.py:16
  619.0 31.3 %all-gather = f32[16,1,8192]{2,1,0:T(1,128)S(1)} all-gather(f32[1,1,8192]{2,1,0:T(1,128)S(1)} %reshape.235), channel_id=1, replica_groups=mesh['parts'=2,'rows'=2,'cols'=8] {'rows','cols'}, dimensions={0}, use_global_device_ids=true | all-gather | bytes 557056 | tf_op jit(solution)/shard_map/all_gather | solution.py:16
  (1234 shorter events, 381.2 us)
Async XLA Ops:
  7.2 47.8 %all-gather.4.cloned.1.call-start = ((), (), s32[]{:S(2)}) async-start(), calls=%async_computation | async-start | bytes 1474560 | tf_op jit(solution)/shard_map/all_gather | solution.py:34
  55.0 2.0 copy-start
  57.1 0.9 copy-start.1
Sparse Core Ops, SparseCore 0:
  10.2 44.7 all-gather.3
where the time goes:
time: 665 us; the launch traced here: 661 us
  matrix products  261 us (39%)
  other arithmetic  144 us (22%)
  blocking collectives  79.9 us (12%)
  loops' own time  60.7 us (9%)
  local copies, waits for them, and re-layouts  54.4 us (8%)
  waiting for transfers between devices  46.1 us (7%)
  between operations  14.2 us (2%)
    dot_general x92, matrix products, take_group(): jnp.einsum('dr,gdc->rgc', xs, group[:, :D, :], precision=lax.Precision.HI...  239 us
    all_gather x2, blocking collectives, joined(): everything = jax.tree.map(lambda part: lax.all_gather(part, axis), array)  79.9 us
    lt x92, other arithmetic, take_group(): mask = jnp.repeat(step * GROUP + within < count, BLK)  63.9 us
    another operation x1, loops' own time, on_device(): lax.scan(row_step, init, jnp.arange(pairs.shape[0], dtype=jnp.int32))  53.5 us
    all_gather x1, waiting for transfers between devices, on_device(): whole = lax.all_gather(packed, 'cols', axis=1, tiled=True)  46.1 us
    reduce_sum x46, other arithmetic, row_pass(): jnp.sum(jnp.exp(scores - top[:, None]), axis=1)  16.6 us
    reduce_sum x46, other arithmetic, col_pass(): jnp.sum(jnp.exp(scores - col_top[None, :]), axis=0)  13.5 us
    select_n x32, other arithmetic, row_step(): slabs = jnp.take(blocks, row_ids, axis=0)  13.3 us
  transfers between devices with their start and end apart: 1, of which 1 were waited for; matrix products, arithmetic and copies ran while one was open for 0% of the time, Pallas kernels for 0%

commit v1 on v0

v1 whole, which is shorter than its diff:
```python
import functools

import jax
import jax.numpy as jnp
from jax import lax
from jax.experimental import pallas as pl
from jax.experimental.pallas import tpu as pltpu
from jax.sharding import PartitionSpec as P

BLK = 256
KP = 256
LANE = 128

epsilon = 0.1
NEG = -1e30
LOG2E = 1.4426950408889634
LN2 = 0.6931471805599453


def split3(v):
    first = lax.reduce_precision(v, exponent_bits=8, mantissa_bits=7)
    rest = v - first
    second = lax.reduce_precision(rest, exponent_bits=8, mantissa_bits=7)
    third = rest - second
    return (first.astype(jnp.bfloat16), second.astype(jnp.bfloat16),
            third.astype(jnp.bfloat16))


def split3_kernel(v):
    first = v.astype(jnp.bfloat16)
    rest = v - first.astype(jnp.float32)
    second = rest.astype(jnp.bfloat16)
    third = (rest - second.astype(jnp.float32)).astype(jnp.bfloat16)
    return first, second, third


def build_table(d, blocks_ref, tab_ref):
    scale = 2.0 * LOG2E / epsilon
    slot_row = lax.broadcasted_iota(jnp.int32, (16, BLK), 0)
    used = 6 * d + 16

    def one(tb, carry):
        blk = blocks_ref[tb]
        y = blk[0:d, :]
        yn = jnp.sum(y * y, axis=0, keepdims=True)
        tp = blk[d:d + 1, :]
        lt = blk[d + 1:d + 2, :]
        acol = (lt + (tp - yn) / epsilon) * LOG2E
        ccol = (-yn / epsilon) * LOG2E
        y1, y2, y3 = split3_kernel(y * scale)
        for k, piece in enumerate([y1, y2, y1, y3, y2, y1]):
            tab_ref[tb, k * d:(k + 1) * d, :] = piece
        slot = jnp.zeros((16, BLK), jnp.float32)
        pieces = list(split3_kernel(acol)) + list(split3_kernel(ccol))
        for k, piece in enumerate(pieces):
            slot = jnp.where(slot_row == k, piece.astype(jnp.float32), slot)
        slot = jnp.where((slot_row >= 6) & (slot_row < 9), 1.0, slot)
        tab_ref[tb, 6 * d:used, :] = slot.astype(jnp.bfloat16)
        tab_ref[tb, used:KP, :] = jnp.zeros((KP - used, BLK), jnp.bfloat16)
        return carry

    lax.fori_loop(0, tab_ref.shape[0], one, 0)


def sinkhorn_kernel(npairs, d, pairs_ref, counts_ref, xt_ref, xn_ref, ls_ref, expand_ref, sel_ref,
                    blocks_ref, fpot_ref, gtop_ref, gsum_ref, sbuf, xr_ref, xc_ref, acc_ref, tab_ref):
    b = pl.program_id(0)

    @pl.when(b == 0)
    def _init():
        gtop_ref[...] = jnp.full(gtop_ref.shape, NEG, jnp.float32)
        gsum_ref[...] = jnp.zeros(gsum_ref.shape, jnp.float32)
        build_table(d, blocks_ref, tab_ref)

    cnt = counts_ref[b]
    base = b * npairs
    x1, x2, x3 = split3_kernel(xt_ref[...])
    xa = (jnp.dot(x1, expand_ref[0], preferred_element_type=jnp.float32)
          + jnp.dot(x2, expand_ref[1], preferred_element_type=jnp.float32)
          + jnp.dot(x3, expand_ref[2], preferred_element_type=jnp.float32))
    sel = sel_ref[...]
    xr_ref[...] = (xa + sel[0:1, :]).astype(jnp.bfloat16)
    acc_ref[...] = jnp.full(acc_ref.shape, NEG, jnp.float32)

    def pairs_of(body):
        def two(k, carry):
            body([2 * k, 2 * k + 1])
            return carry

        lax.fori_loop(0, cnt // 2, two, 0)

        @pl.when(cnt % 2 == 1)
        def _last():
            body([cnt - 1])

    def row_max(ts):
        best = None
        for t in ts:
            s = jnp.dot(xr_ref[...], tab_ref[pairs_ref[base + t]], preferred_element_type=jnp.float32)
            sbuf[t] = s
            half = jnp.maximum(s[:, :LANE], s[:, LANE:])
            best = half if best is None else jnp.maximum(best, half)
        acc_ref[...] = jnp.maximum(acc_ref[...], best)

    pairs_of(row_max)
    m = jnp.max(acc_ref[...], axis=1, keepdims=True)
    acc_ref[...] = jnp.zeros(acc_ref.shape, jnp.float32)

    def row_sum(ts):
        total = None
        for t in ts:
            e = jnp.exp2(sbuf[t] - m)
            part = e[:, :LANE] + e[:, LANE:]
            total = part if total is None else total + part
        acc_ref[...] = acc_ref[...] + total

    pairs_of(row_sum)
    lse = m + jnp.log2(jnp.sum(acc_ref[...], axis=1, keepdims=True))
    fpot_ref[...] = xn_ref[...] - (epsilon * LN2) * lse
    p1, p2, p3 = split3_kernel(ls_ref[...] * LOG2E - lse)
    xc_ref[...] = (xa + sel[1:2, :] + p1.astype(jnp.float32) * sel[2:3, :]
                   + p2.astype(jnp.float32) * sel[3:4, :]
                   + p3.astype(jnp.float32) * sel[4:5, :]).astype(jnp.bfloat16)

    def col_pass(ts):
        for t in ts:
            tb = pairs_ref[base + t]
            u = jnp.dot(xc_ref[...], tab_ref[tb], preferred_element_type=jnp.float32)
            sbuf[t] = u
            cm = jnp.max(u, axis=0, keepdims=True)
            cs = jnp.sum(jnp.exp2(sbuf[t] - cm), axis=0, keepdims=True)
            old = gtop_ref[tb]
            new = jnp.maximum(old, cm)
            gsum_ref[tb] = gsum_ref[tb] * jnp.exp2(old - new) + cs * jnp.exp2(cm - new)
            gtop_ref[tb] = new

    pairs_of(col_pass)


def merge(tops, sums, axis):
    top = jnp.max(tops, axis=axis, keepdims=True)
    total = jnp.sum(sums * jnp.exp2(tops - top), axis=axis, keepdims=True)
    return top, total


def on_device(src_feat, tgt_feat, tgt_pot, log_src, log_tgt, pairs, counts):
    d = src_feat.shape[0]
    ns = src_feat.shape[1]
    nrb = ns // BLK
    npairs = pairs.shape[1]
    own_targets = tgt_feat.shape[1]
    ncols = lax.axis_size("cols")

    packed = jnp.concatenate([tgt_feat, tgt_pot[None, :], log_tgt[None, :]], axis=0)
    rowsp = packed.shape[0]
    spread = jnp.broadcast_to(packed[None], (ncols, rowsp, own_targets))
    gathered = lax.all_to_all(spread, "cols", 0, 0, tiled=True)
    nt = ncols * own_targets
    tblocks = nt // BLK
    blocks = jnp.transpose(
        gathered.reshape(ncols, rowsp, own_targets // BLK, BLK), (0, 2, 1, 3)).reshape(tblocks, rowsp, BLK)

    col = jnp.arange(KP, dtype=jnp.int32)[None, :]
    comp = jnp.arange(d, dtype=jnp.int32)[:, None]
    def place(starts):
        hit = jnp.zeros((d, KP), bool)
        for s in starts:
            hit = hit | (col == comp + s)
        return hit.astype(jnp.bfloat16)
    expand = jnp.stack([place([0, d, 3 * d]), place([2 * d, 4 * d]), place([5 * d])])
    k0 = 6 * d
    sel = jnp.stack([
        ((col[0] >= k0) & (col[0] < k0 + 3)),
        ((col[0] >= k0 + 3) & (col[0] < k0 + 6)),
        col[0] == k0 + 6, col[0] == k0 + 7, col[0] == k0 + 8,
        col[0] < 0, col[0] < 0, col[0] < 0,
    ]).astype(jnp.float32)

    xt = jnp.transpose(src_feat)
    xn = jnp.sum(src_feat * src_feat, axis=0)[:, None]
    ls = log_src[:, None]

    grid_spec = pltpu.PrefetchScalarGridSpec(
        num_scalar_prefetch=2,
        grid=(nrb,),
        in_specs=[
            pl.BlockSpec((BLK, d), lambda b, pr, ct: (b, 0)),
            pl.BlockSpec((BLK, 1), lambda b, pr, ct: (b, 0)),
            pl.BlockSpec((BLK, 1), lambda b, pr, ct: (b, 0)),
            pl.BlockSpec((3, d, KP), lambda b, pr, ct: (0, 0, 0)),
            pl.BlockSpec((8, KP), lambda b, pr, ct: (0, 0)),
            pl.BlockSpec((tblocks, rowsp, BLK), lambda b, pr, ct: (0, 0, 0)),
        ],
        out_specs=[
            pl.BlockSpec((BLK, 1), lambda b, pr, ct: (b, 0)),
            pl.BlockSpec((tblocks, 1, BLK), lambda b, pr, ct: (0, 0, 0)),
            pl.BlockSpec((tblocks, 1, BLK), lambda b, pr, ct: (0, 0, 0)),
        ],
        scratch_shapes=[pltpu.VMEM((npairs, BLK, BLK), jnp.float32),
                        pltpu.VMEM((BLK, KP), jnp.bfloat16),
                        pltpu.VMEM((BLK, KP), jnp.bfloat16),
                        pltpu.VMEM((BLK, LANE), jnp.float32),
                        pltpu.VMEM((tblocks, KP, BLK), jnp.bfloat16)],
    )
    fpot, gtop, gsum = pl.pallas_call(
        functools.partial(sinkhorn_kernel, npairs, d),
        grid_spec=grid_spec,
        out_shape=[
            jax.ShapeDtypeStruct((ns, 1), jnp.float32),
            jax.ShapeDtypeStruct((tblocks, 1, BLK), jnp.float32),
            jax.ShapeDtypeStruct((tblocks, 1, BLK), jnp.float32),
        ],
        compiler_params=pltpu.CompilerParams(
            dimension_semantics=("arbitrary",), vmem_limit_bytes=100 * 1024 * 1024),
    )(pairs.reshape(-1), counts, xt, xn, ls, expand, sel, blocks)

    src_pot = fpot.reshape(-1)
    parts = jnp.stack([gtop.reshape(ncols, own_targets), gsum.reshape(ncols, own_targets)], axis=1)
    mine = lax.all_to_all(parts, "cols", 0, 0, tiled=True)
    top, total = merge(mine[:, 0, :], mine[:, 1, :], 0)
    both = lax.all_gather(jnp.concatenate([top, total], axis=0), "rows")
    top, total = merge(both[:, 0, :], both[:, 1, :], 0)
    new_tgt_pot = (-epsilon * LN2) * (top[0] + jnp.log2(total[0]))
    return (src_pot, new_tgt_pot)


def solution(mesh):
    placed = (
        P(None, ("parts", "rows", "cols")),
        P(None, ("parts", "cols")),
        P(("parts", "cols")),
        P(("parts", "rows", "cols")),
        P(("parts", "cols")),
        P(("parts", "rows", "cols"), None),
        P(("parts", "rows", "cols")),
    )
    return jax.shard_map(
        on_device,
        mesh=mesh,
        in_specs=placed,
        out_specs=(P(("parts", "rows", "cols")), P(("parts", "cols"))),
        check_vma=False,
    )
```

time: 665 us -> 194 us (0.29)
  the two profiles are of different devices: /device:TPU:0 before, /device:TPU:3 now
where the time goes in v1:
time: 194 us; the launch traced here: 193 us
  Pallas kernels  121 us (62%)
  starting transfers between devices  28.1 us (14%)
  waiting for transfers between devices  25.2 us (13%)
  local copies, waits for them, and re-layouts  9.25 us (5%)
  other arithmetic  7.66 us (4%)
    pallas_call x1, Pallas kernels, on_device(): pl.pallas_call(functools.partial(sinkhorn_kernel, npairs, d), grid_spec=g...  121 us
    all_to_all x1, starting transfers between devices, on_device(): mine = lax.all_to_all(parts, 'cols', 0, 0, tiled=True)  22.4 us
    all_to_all x1, waiting for transfers between devices, on_device(): gathered = lax.all_to_all(spread, 'cols', 0, 0, tiled=True)  22.3 us
    all_to_all x1, starting transfers between devices, on_device(): gathered = lax.all_to_all(spread, 'cols', 0, 0, tiled=True)  5.69 us
  transfers between devices with their start and end apart: 2, of which 2 were waited for; matrix products, arithmetic and copies ran while one was open for 6% of the time, Pallas kernels for 0%

profile of v1, /device:TPU:3, one launch (start us, length us, event | category | flops | bytes accessed | tf_op | source)
XLA Modules:
  0.0 193.4 jit_solution(3897377241983925399)
XLA Ops:
  0.6 1.0 pad_maximum_fusion.1
  1.6 1.2 broadcast_in_dim.31
  2.8 0.0 copy-start.2
  2.8 0.0 copy-start
  2.8 5.7 %all-to-all-start = ((f32[8,34,1024]{2,1,0:T(8,128)}), f32[8,34,1024]{2,1,0:T(8,128)S(1)}, u32[]{:S(2)}, u32[]{:S(2)}) async-start(f32[8,34,1024]{2,1,0:T(8,128)} %broadcast_in_dim.31), calls=%async_computation | async-start | bytes 2621440 | tf_op jit(solution)/shard_map/all_to_all | solution.py:157
  8.5 0.0 copy-done.2
  8.5 0.7 reshape.274.pairs_ref
  9.3 0.6 convert_element_type.27.sel_ref
  9.9 0.0 copy-done
  9.9 2.0 %copy.15 = f32[32,4096]{0,1:T(8,128)} copy(f32[32,4096]{1,0:T(8,128)S(1)} %copy-done) | data formatting | bytes 1048576 | tf_op args[0]
  11.8 0.0 copy-start.1
  11.8 0.1 multiply_reduce_fusion
  11.9 1.9 %copy.16.xn_ref = f32[4096,1]{1,0:T(8,128)} copy(f32[4096,1]{0,1:T(1,128)S(1)} %bitcast.40) | data formatting | bytes 32768 | tf_op jit(solution)/shard_map/broadcast_in_dim | solution.py:180
  13.9 0.0 copy-done.1
  13.9 2.0 %copy.17.ls_ref = f32[4096,1]{1,0:T(8,128)} copy(f32[4096,1]{0,1:T(1,128)S(1)} %bitcast.44) | data formatting | bytes 32768 | tf_op jit(solution)/shard_map/broadcast_in_dim | solution.py:181
  15.9 0.1 iota_compare_fusion
  15.9 0.1 fusion.7
  16.0 0.1 fusion.6
  16.1 0.6 add_convert_fusion.expand_ref
  16.7 22.3 %all-to-all-done = f32[8,34,1024]{2,1,0:T(8,128)S(1)} async-done(((f32[8,34,1024]{2,1,0:T(8,128)}), f32[8,34,1024]{2,1,0:T(8,128)S(1)}, u32[]{:S(2)}, u32[]{:S(2)}) %all-to-all-start) | async-done | bytes 1114144 | tf_op jit(solution)/shard_map/all_to_all | solution.py:157
  39.0 0.1 fusion.12
  39.1 0.1 pad_maximum_fusion
  39.3 1.3 reshape.275.blocks_ref
  40.6 120.6 %shard_map.86 = (f32[4096,1]{1,0:T(8,128)}, f32[32,1,256]{2,1,0:T(1,128)}, f32[32,1,256]{2,1,0:T(1,128)}) custom-call(s32[384]{0:T(512)} %reshape.274.pairs_ref, s32[16]{0:T(128)} %counts_ref.1, f32[4096,32]{1,0:T(8,128)} %bitcast.39, f32[4096,1]{1,0:T(8,128)} %copy.16.xn_ref, f32[4096,1]{1,0:T(8,128)} %copy.17.ls_ref, ...), custom_call_target="tpu_custom_call" | custom-call | tf_op jit(solution)/shard_map/pallas_call | solution.py:205
  161.2 1.5 pad_maximum_fusion.2
  162.6 22.4 %all-to-all-start.1 = ((f32[8,2,1024]{2,1,0:T(2,128)}), f32[8,2,1024]{2,1,0:T(2,128)S(1)}, u32[]{:S(2)}, u32[]{:S(2)}) async-start(f32[8,2,1024]{2,1,0:T(2,128)} %pad_maximum_fusion.2), calls=%async_computation.1 | async-start | bytes 131072 | tf_op jit(solution)/shard_map/all_to_all | solution.py:219
  185.0 2.8 %reduce.2 = f32[4096]{0:T(1024)} reduce(f32[4096,1]{1,0:T(8,128)} %get-tuple-element.5, f32[]{:T(128)} %constant.36), dimensions={1}, to_apply=%get-tuple-element.5.reduce_sub_computation | reduce | bytes 32772 | tf_op jit(solution)/shard_map/pallas_call | solution.py:205
  187.8 2.9 %all-to-all-done.1 = f32[8,2,1024]{2,1,0:T(2,128)S(1)} async-done(((f32[8,2,1024]{2,1,0:T(2,128)}), f32[8,2,1024]{2,1,0:T(2,128)S(1)}, u32[]{:S(2)}, u32[]{:S(2)}) %all-to-all-start.1) | async-done | bytes 65568 | tf_op jit(solution)/shard_map/all_to_all | solution.py:219
  190.8 0.1 slice_reduce_fusion.1
  190.9 1.8 all-gather.1
  192.8 0.6 add_multiply_fusion
  (12 shorter events, 0.2 us)
Async XLA Ops:
  2.8 5.7 %copy-start.2 = (s32[16,24]{1,0:T(8,128)S(1)}, s32[16,24]{1,0:T(8,128)}, u32[]{:S(2)}) copy-start(s32[16,24]{1,0:T(8,128)} %param.12) | copy-start | bytes 4612
  2.8 7.1 %copy-start = (f32[32,4096]{1,0:T(8,128)S(1)}, f32[32,4096]{1,0:T(8,128)}, u32[]{:S(2)}) copy-start(f32[32,4096]{1,0:T(8,128)} %param.7) | copy-start | bytes 1572868
  2.8 36.2 %all-to-all-start = ((f32[8,34,1024]{2,1,0:T(8,128)}), f32[8,34,1024]{2,1,0:T(8,128)S(1)}, u32[]{:S(2)}, u32[]{:S(2)}) async-start(f32[8,34,1024]{2,1,0:T(8,128)} %broadcast_in_dim.31), calls=%async_computation | async-start | bytes 2621440 | tf_op jit(solution)/shard_map/all_to_all | solution.py:157
  11.8 2.0 %copy-start.1 = (f32[4096]{0:T(1024)S(1)}, f32[4096]{0:T(1024)}, u32[]{:S(2)}) copy-start(f32[4096]{0:T(1024)} %param.10) | copy-start | bytes 49156
  162.6 28.1 %all-to-all-start.1 = ((f32[8,2,1024]{2,1,0:T(2,128)}), f32[8,2,1024]{2,1,0:T(2,128)S(1)}, u32[]{:S(2)}, u32[]{:S(2)}) async-start(f32[8,2,1024]{2,1,0:T(2,128)} %pad_maximum_fusion.2), calls=%async_computation.1 | async-start | bytes 131072 | tf_op jit(solution)/shard_map/all_to_all | solution.py:219

commit v2 on v1

--- a/solution.py
+++ b/solution.py
@@ -80,7 +80,8 @@
           + jnp.dot(x3, expand_ref[2], preferred_element_type=jnp.float32))
     sel = sel_ref[...]
     xr_ref[...] = (xa + sel[0:1, :]).astype(jnp.bfloat16)
-    acc_ref[...] = jnp.full(acc_ref.shape, NEG, jnp.float32)
+    acc_ref[0] = jnp.full((BLK, LANE), NEG, jnp.float32)
+    acc_ref[1] = jnp.zeros((BLK, LANE), jnp.float32)
 
     def pairs_of(body):
         def two(k, carry):
@@ -93,29 +94,26 @@
         def _last():
             body([cnt - 1])
 
-    def row_max(ts):
-        best = None
+    def row_pass(ts):
+        halves = []
         for t in ts:
             s = jnp.dot(xr_ref[...], tab_ref[pairs_ref[base + t]], preferred_element_type=jnp.float32)
-            sbuf[t] = s
-            half = jnp.maximum(s[:, :LANE], s[:, LANE:])
-            best = half if best is None else jnp.maximum(best, half)
-        acc_ref[...] = jnp.maximum(acc_ref[...], best)
-
-    pairs_of(row_max)
-    m = jnp.max(acc_ref[...], axis=1, keepdims=True)
-    acc_ref[...] = jnp.zeros(acc_ref.shape, jnp.float32)
-
-    def row_sum(ts):
-        total = None
-        for t in ts:
-            e = jnp.exp2(sbuf[t] - m)
-            part = e[:, :LANE] + e[:, LANE:]
-            total = part if total is None else total + part
-        acc_ref[...] = acc_ref[...] + total
-
-    pairs_of(row_sum)
-    lse = m + jnp.log2(jnp.sum(acc_ref[...], axis=1, keepdims=True))
+            halves += [s[:, :LANE], s[:, LANE:]]
+        old = acc_ref[0]
+        new = old
+        for h in halves:
+            new = jnp.maximum(new, h)
+        total = acc_ref[1] * jnp.exp2(old - new)
+        for h in halves:
+            total = total + jnp.exp2(h - new)
+        acc_ref[0] = new
+        acc_ref[1] = total
+
+    pairs_of(row_pass)
+    lane_top = acc_ref[0]
+    m = jnp.max(lane_top, axis=1, keepdims=True)
+    lane_sum = acc_ref[1] * jnp.exp2(lane_top - m)
+    lse = m + jnp.log2(jnp.sum(lane_sum, axis=1, keepdims=True))
     fpot_ref[...] = xn_ref[...] - (epsilon * LN2) * lse
     p1, p2, p3 = split3_kernel(ls_ref[...] * LOG2E - lse)
     xc_ref[...] = (xa + sel[1:2, :] + p1.astype(jnp.float32) * sel[2:3, :]
@@ -123,12 +121,12 @@
                    + p3.astype(jnp.float32) * sel[4:5, :]).astype(jnp.bfloat16)
 
     def col_pass(ts):
-        for t in ts:
+        for slot, t in enumerate(ts):
             tb = pairs_ref[base + t]
             u = jnp.dot(xc_ref[...], tab_ref[tb], preferred_element_type=jnp.float32)
-            sbuf[t] = u
+            sbuf[slot] = u
             cm = jnp.max(u, axis=0, keepdims=True)
-            cs = jnp.sum(jnp.exp2(sbuf[t] - cm), axis=0, keepdims=True)
+            cs = jnp.sum(jnp.exp2(sbuf[slot] - cm), axis=0, keepdims=True)
             old = gtop_ref[tb]
             new = jnp.maximum(old, cm)
             gsum_ref[tb] = gsum_ref[tb] * jnp.exp2(old - new) + cs * jnp.exp2(cm - new)
@@ -196,10 +194,10 @@
             pl.BlockSpec((tblocks, 1, BLK), lambda b, pr, ct: (0, 0, 0)),
             pl.BlockSpec((tblocks, 1, BLK), lambda b, pr, ct: (0, 0, 0)),
         ],
-        scratch_shapes=[pltpu.VMEM((npairs, BLK, BLK), jnp.float32),
+        scratch_shapes=[pltpu.VMEM((2, BLK, BLK), jnp.float32),
                         pltpu.VMEM((BLK, KP), jnp.bfloat16),
                         pltpu.VMEM((BLK, KP), jnp.bfloat16),
-                        pltpu.VMEM((BLK, LANE), jnp.float32),
+                        pltpu.VMEM((2, BLK, LANE), jnp.float32),
                         pltpu.VMEM((tblocks, KP, BLK), jnp.bfloat16)],
     )
     fpot, gtop, gsum = pl.pallas_call(

time: 194 us -> 186 us (0.959)
  starting transfers between devices: 28.1 us -> 12.6 us
  blocking collectives: 1.81 us -> 6.21 us
  Pallas kernels: 121 us -> 123 us
    all_to_all x1, starting transfers between devices: 22.4 us -> 6.88 us  [on_device(): mine = lax.all_to_all(parts, 'cols', 0, 0, tiled=True)]
    all_gather x1, blocking collectives: 1.81 us -> 6.21 us  [on_device(): both = lax.all_gather(jnp.concatenate([top, total], axis=0), 'rows')]
    pallas_call x1, Pallas kernels: 121 us -> 123 us  [on_device(): pl.pallas_call(functools.partial(sinkhorn_kernel, npairs, d), grid_spec=g...]
where the time goes in v2:
time: 186 us; the launch traced here: 185 us
  Pallas kernels  123 us (66%)
  waiting for transfers between devices  25.2 us (14%)
  starting transfers between devices  12.6 us (7%)
  local copies, waits for them, and re-layouts  9.25 us (5%)
  other arithmetic  7.66 us (4%)
  blocking collectives  6.21 us (3%)
    pallas_call x1, Pallas kernels, on_device(): pl.pallas_call(functools.partial(sinkhorn_kernel, npairs, d), grid_spec=g...  123 us
    all_to_all x1, waiting for transfers between devices, on_device(): gathered = lax.all_to_all(spread, 'cols', 0, 0, tiled=True)  22.3 us
    all_to_all x1, starting transfers between devices, on_device(): mine = lax.all_to_all(parts, 'cols', 0, 0, tiled=True)  6.88 us
    all_gather x1, blocking collectives, on_device(): both = lax.all_gather(jnp.concatenate([top, total], axis=0), 'rows')  6.21 us
    all_to_all x1, starting transfers between devices, on_device(): gathered = lax.all_to_all(spread, 'cols', 0, 0, tiled=True)  5.69 us
  transfers between devices with their start and end apart: 2, of which 2 were waited for; matrix products, arithmetic and copies ran while one was open for 6% of the time, Pallas kernels for 0%

profile of v2, /device:TPU:3, one launch (start us, length us, event | category | flops | bytes accessed | tf_op | source)
XLA Modules:
  0.0 184.5 jit_solution(5308289643535955034)
XLA Ops:
  0.6 1.0 pad_maximum_fusion.1
  1.6 1.2 broadcast_in_dim.31
  2.8 0.0 copy-start.2
  2.8 0.0 copy-start
  2.8 5.7 %all-to-all-start = ((f32[8,34,1024]{2,1,0:T(8,128)}), f32[8,34,1024]{2,1,0:T(8,128)S(1)}, u32[]{:S(2)}, u32[]{:S(2)}) async-start(f32[8,34,1024]{2,1,0:T(8,128)} %broadcast_in_dim.31), calls=%async_computation | async-start | bytes 2621440 | tf_op jit(solution)/shard_map/all_to_all | solution.py:155
  8.5 0.0 copy-done.2
  8.5 0.7 reshape.274.pairs_ref
  9.3 0.6 convert_element_type.27.sel_ref
  9.9 0.0 copy-done
  9.9 2.0 %copy.15 = f32[32,4096]{0,1:T(8,128)} copy(f32[32,4096]{1,0:T(8,128)S(1)} %copy-done) | data formatting | bytes 1048576 | tf_op args[0]
  11.8 0.0 copy-start.1
  11.8 0.1 multiply_reduce_fusion
  11.9 1.9 %copy.16.xn_ref = f32[4096,1]{1,0:T(8,128)} copy(f32[4096,1]{0,1:T(1,128)S(1)} %bitcast.40) | data formatting | bytes 32768 | tf_op jit(solution)/shard_map/broadcast_in_dim | solution.py:178
  13.9 0.0 copy-done.1
  13.9 2.0 %copy.17.ls_ref = f32[4096,1]{1,0:T(8,128)} copy(f32[4096,1]{0,1:T(1,128)S(1)} %bitcast.44) | data formatting | bytes 32768 | tf_op jit(solution)/shard_map/broadcast_in_dim | solution.py:179
  15.9 0.1 iota_compare_fusion
  15.9 0.1 fusion.7
  16.0 0.1 fusion.6
  16.1 0.6 add_convert_fusion.expand_ref
  16.7 22.3 %all-to-all-done = f32[8,34,1024]{2,1,0:T(8,128)S(1)} async-done(((f32[8,34,1024]{2,1,0:T(8,128)}), f32[8,34,1024]{2,1,0:T(8,128)S(1)}, u32[]{:S(2)}, u32[]{:S(2)}) %all-to-all-start) | async-done | bytes 1114144 | tf_op jit(solution)/shard_map/all_to_all | solution.py:155
  39.0 0.1 fusion.12
  39.1 0.1 pad_maximum_fusion
  39.3 1.3 reshape.275.blocks_ref
  40.6 122.9 %shard_map.86 = (f32[4096,1]{1,0:T(8,128)}, f32[32,1,256]{2,1,0:T(1,128)}, f32[32,1,256]{2,1,0:T(1,128)}) custom-call(s32[384]{0:T(512)} %reshape.274.pairs_ref, s32[16]{0:T(128)} %counts_ref.1, f32[4096,32]{1,0:T(8,128)} %bitcast.39, f32[4096,1]{1,0:T(8,128)} %copy.16.xn_ref, f32[4096,1]{1,0:T(8,128)} %copy.17.ls_ref, ...), custom_call_target="tpu_custom_call" | custom-call | tf_op jit(solution)/shard_map/pallas_call | solution.py:203
  163.4 1.5 pad_maximum_fusion.2
  164.9 6.9 %all-to-all-start.1 = ((f32[8,2,1024]{2,1,0:T(2,128)}), f32[8,2,1024]{2,1,0:T(2,128)S(1)}, u32[]{:S(2)}, u32[]{:S(2)}) async-start(f32[8,2,1024]{2,1,0:T(2,128)} %pad_maximum_fusion.2), calls=%async_computation.1 | async-start | bytes 131072 | tf_op jit(solution)/shard_map/all_to_all | solution.py:217
  171.8 2.8 %reduce.2 = f32[4096]{0:T(1024)} reduce(f32[4096,1]{1,0:T(8,128)} %get-tuple-element.5, f32[]{:T(128)} %constant.36), dimensions={1}, to_apply=%get-tuple-element.5.reduce_sub_computation | reduce | bytes 32772 | tf_op jit(solution)/shard_map/pallas_call | solution.py:203
  174.6 2.9 %all-to-all-done.1 = f32[8,2,1024]{2,1,0:T(2,128)S(1)} async-done(((f32[8,2,1024]{2,1,0:T(2,128)}), f32[8,2,1024]{2,1,0:T(2,128)S(1)}, u32[]{:S(2)}, u32[]{:S(2)}) %all-to-all-start.1) | async-done | bytes 65568 | tf_op jit(solution)/shard_map/all_to_all | solution.py:217
  177.5 0.1 slice_reduce_fusion.1
  177.7 6.2 %all-gather.1 = f32[2,2,1024]{2,1,0:T(2,128)S(1)} all-gather(f32[1,2,1024]{2,1,0:T(2,128)S(1)} %maximum_bitcast_fusion), channel_id=2, replica_groups=mesh['parts'=2,'rows'=2,'cols'=8] {'rows'}, dimensions={0}, use_global_device_ids=true | all-gather | bytes 24576 | tf_op jit(solution)/shard_map/all_gather | solution.py:219
  183.9 0.6 add_multiply_fusion
  (12 shorter events, 0.2 us)
Async XLA Ops:
  2.8 5.7 %copy-start.2 = (s32[16,24]{1,0:T(8,128)S(1)}, s32[16,24]{1,0:T(8,128)}, u32[]{:S(2)}) copy-start(s32[16,24]{1,0:T(8,128)} %param.12) | copy-start | bytes 4612
  2.8 7.1 %copy-start = (f32[32,4096]{1,0:T(8,128)S(1)}, f32[32,4096]{1,0:T(8,128)}, u32[]{:S(2)}) copy-start(f32[32,4096]{1,0:T(8,128)} %param.7) | copy-start | bytes 1572868
  2.8 36.2 %all-to-all-start = ((f32[8,34,1024]{2,1,0:T(8,128)}), f32[8,34,1024]{2,1,0:T(8,128)S(1)}, u32[]{:S(2)}, u32[]{:S(2)}) async-start(f32[8,34,1024]{2,1,0:T(8,128)} %broadcast_in_dim.31), calls=%async_computation | async-start | bytes 2621440 | tf_op jit(solution)/shard_map/all_to_all | solution.py:155
  11.8 2.0 %copy-start.1 = (f32[4096]{0:T(1024)S(1)}, f32[4096]{0:T(1024)}, u32[]{:S(2)}) copy-start(f32[4096]{0:T(1024)} %param.10) | copy-start | bytes 49156
  164.9 12.6 %all-to-all-start.1 = ((f32[8,2,1024]{2,1,0:T(2,128)}), f32[8,2,1024]{2,1,0:T(2,128)S(1)}, u32[]{:S(2)}, u32[]{:S(2)}) async-start(f32[8,2,1024]{2,1,0:T(2,128)} %pad_maximum_fusion.2), calls=%async_computation.1 | async-start | bytes 131072 | tf_op jit(solution)/shard_map/all_to_all | solution.py:217

commit v3 on v2

--- a/solution.py
+++ b/solution.py
@@ -151,8 +151,12 @@
 
     packed = jnp.concatenate([tgt_feat, tgt_pot[None, :], log_tgt[None, :]], axis=0)
     rowsp = packed.shape[0]
-    spread = jnp.broadcast_to(packed[None], (ncols, rowsp, own_targets))
-    gathered = lax.all_to_all(spread, "cols", 0, 0, tiled=True)
+    nrows = lax.axis_size("rows")
+    share = rowsp // nrows
+    mine = lax.dynamic_slice_in_dim(packed, lax.axis_index("rows") * share, share, 0)
+    spread = jnp.broadcast_to(mine[None], (ncols, share, own_targets))
+    halves = lax.all_to_all(spread, "cols", 0, 0, tiled=True)
+    gathered = lax.all_gather(halves, "rows", axis=1, tiled=True)
     nt = ncols * own_targets
     tblocks = nt // BLK
     blocks = jnp.transpose(

time: 186 us -> 201 us (1.081)
  the two profiles are of different devices: /device:TPU:3 before, /device:TPU:0 now
where the time goes in v3:
time: 201 us
  Pallas kernels  82.1 us (41%)
  starting transfers between devices  48.5 us (24%)
  waiting for transfers between devices  24.2 us (12%)
  between operations  14.2 us (7%)
  blocking collectives  12.2 us (6%)
  local copies, waits for them, and re-layouts  11.7 us (6%)
  other arithmetic  7.64 us (4%)
    pallas_call x1, Pallas kernels, on_device(): pl.pallas_call(functools.partial(sinkhorn_kernel, npairs, d), grid_spec=g...  82.1 us
    all_to_all x1, starting transfers between devices, on_device(): mine = lax.all_to_all(parts, 'cols', 0, 0, tiled=True)  41.1 us
    all_to_all x1, waiting for transfers between devices, on_device(): halves = lax.all_to_all(spread, 'cols', 0, 0, tiled=True)  12.8 us
    all_gather x1, blocking collectives, on_device(): both = lax.all_gather(jnp.concatenate([top, total], axis=0), 'rows')  12.2 us
    all_gather x1, waiting for transfers between devices, on_device(): gathered = lax.all_gather(halves, 'rows', axis=1, tiled=True)  7.32 us
    all_to_all x1, starting transfers between devices, on_device(): halves = lax.all_to_all(spread, 'cols', 0, 0, tiled=True)  7.28 us
    all_to_all x1, waiting for transfers between devices, on_device(): mine = lax.all_to_all(parts, 'cols', 0, 0, tiled=True)  4.09 us
  transfers between devices with their start and end apart: 3, of which 3 were waited for; matrix products, arithmetic and copies ran while one was open for 5% of the time, Pallas kernels for 0%

profile of v3, /device:TPU:0, one launch (start us, length us, event | category | flops | bytes accessed | tf_op | source)
XLA Modules:
  0.0 200.5 jit_solution(2241050458972396731)
XLA Ops:
  7.2 1.0 fusion.1
  8.1 0.0 copy-start.2
  8.2 0.0 copy-start
  8.2 1.0 broadcast_in_dim.31
  9.1 7.3 %all-to-all-start = ((f32[8,17,1024]{2,1,0:T(8,128)}), f32[8,17,1024]{2,1,0:T(8,128)S(1)}, u32[]{:S(2)}, u32[]{:S(2)}) async-start(f32[8,17,1024]{2,1,0:T(8,128)} %broadcast_in_dim.31), calls=%async_computation | async-start | bytes 1572864 | tf_op jit(solution)/shard_map/all_to_all | solution.py:158
  16.4 0.0 all-gather.4.cloned.1.call-start
  16.5 0.0 copy-done.2
  16.5 0.7 reshape.274.pairs_ref
  17.2 0.6 convert_element_type.27.sel_ref
  17.8 0.0 copy-done
  17.8 2.0 copy.23
  19.8 0.1 multiply_reduce_fusion
  19.9 0.0 copy-start.1
  19.9 2.0 copy.26.xn_ref
  21.8 0.0 copy-done.1
  21.8 2.0 copy.27.ls_ref
  23.8 12.8 %all-to-all-done = f32[8,17,1024]{2,1,0:T(8,128)S(1)} async-done(((f32[8,17,1024]{2,1,0:T(8,128)}), f32[8,17,1024]{2,1,0:T(8,128)S(1)}, u32[]{:S(2)}, u32[]{:S(2)}) %all-to-all-start) | async-done | bytes 557088 | tf_op jit(solution)/shard_map/all_to_all | solution.py:158
  36.6 1.1 copy.24
  37.7 0.0 all-gather.4.cloned.1.call-update
  37.8 0.1 iota_compare_fusion
  37.8 0.1 fusion.9
  37.9 0.1 fusion.8
  38.0 0.6 add_convert_fusion.expand_ref
  38.6 7.3 %all-gather.4.cloned.1.call-done = f32[8,34,1024]{2,0,1:T(8,128)} async-done(((f32[8,17,1024]{2,0,1:T(8,128)}), f32[8,34,1024]{2,0,1:T(8,128)}) %all-gather.4.cloned.1.call-update) | async-done | bytes 1114128 | tf_op jit(solution)/shard_map/all_gather | solution.py:159
  45.9 1.3 fusion.14
  47.2 0.1 pad_maximum_fusion
  47.3 0.4 copy.25
  47.7 1.3 reshape.275.blocks_ref
  49.0 82.1 %shard_map.86 = (f32[4096,1]{1,0:T(8,128)}, f32[32,1,256]{2,1,0:T(1,128)}, f32[32,1,256]{2,1,0:T(1,128)}) custom-call(s32[384]{0:T(512)} %reshape.274.pairs_ref, s32[16]{0:T(128)} %counts_ref.1, f32[4096,32]{1,0:T(8,128)} %bitcast.39, f32[4096,1]{1,0:T(8,128)} %copy.26.xn_ref, f32[4096,1]{1,0:T(8,128)} %copy.27.ls_ref, ...), custom_call_target="tpu_custom_call" | custom-call | tf_op jit(solution)/shard_map/pallas_call | solution.py:207
  131.1 1.5 pad_maximum_fusion.1
  132.6 41.1 %all-to-all-start.1 = ((f32[8,2,1024]{2,1,0:T(2,128)}), f32[8,2,1024]{2,1,0:T(2,128)S(1)}, u32[]{:S(2)}, u32[]{:S(2)}) async-start(f32[8,2,1024]{2,1,0:T(2,128)} %pad_maximum_fusion.1), calls=%async_computation.1 | async-start | bytes 131072 | tf_op jit(solution)/shard_map/all_to_all | solution.py:221
  173.7 2.8 %reduce.2 = f32[4096]{0:T(1024)} reduce(f32[4096,1]{1,0:T(8,128)} %get-tuple-element.5, f32[]{:T(128)} %constant.48), dimensions={1}, to_apply=%get-tuple-element.5.reduce_sub_computation | reduce | bytes 32772 | tf_op jit(solution)/shard_map/pallas_call | solution.py:207
  176.5 4.1 %all-to-all-done.1 = f32[8,2,1024]{2,1,0:T(2,128)S(1)} async-done(((f32[8,2,1024]{2,1,0:T(2,128)}), f32[8,2,1024]{2,1,0:T(2,128)S(1)}, u32[]{:S(2)}, u32[]{:S(2)}) %all-to-all-start.1) | async-done | bytes 65568 | tf_op jit(solution)/shard_map/all_to_all | solution.py:221
  180.6 0.1 slice_reduce_fusion.1
  180.8 12.2 %all-gather.1 = f32[2,2,1024]{2,1,0:T(2,128)S(1)} all-gather(f32[1,2,1024]{2,1,0:T(2,128)S(1)} %maximum_bitcast_fusion), channel_id=2, replica_groups=mesh['parts'=2,'rows'=2,'cols'=8] {'rows'}, dimensions={0}, use_global_device_ids=true | all-gather | bytes 24576 | tf_op jit(solution)/shard_map/all_gather | solution.py:223
  193.1 0.6 add_multiply_fusion
  (12 shorter events, 0.2 us)
Async XLA Ops:
  8.1 8.3 %copy-start.2 = (s32[16,24]{1,0:T(8,128)S(1)}, s32[16,24]{1,0:T(8,128)}, u32[]{:S(2)}) copy-start(s32[16,24]{1,0:T(8,128)} %param.12) | copy-start | bytes 4612
  8.2 9.7 %copy-start = (f32[32,4096]{1,0:T(8,128)S(1)}, f32[32,4096]{1,0:T(8,128)}, u32[]{:S(2)}) copy-start(f32[32,4096]{1,0:T(8,128)} %param.7) | copy-start | bytes 1572868
  9.1 27.4 %all-to-all-start = ((f32[8,17,1024]{2,1,0:T(8,128)}), f32[8,17,1024]{2,1,0:T(8,128)S(1)}, u32[]{:S(2)}, u32[]{:S(2)}) async-start(f32[8,17,1024]{2,1,0:T(8,128)} %broadcast_in_dim.31), calls=%async_computation | async-start | bytes 1572864 | tf_op jit(solution)/shard_map/all_to_all | solution.py:158
  16.4 29.5 %all-gather.4.cloned.1.call-start = ((), (), s32[]{:S(2)}) async-start(), calls=%async_computation.2 | async-start | bytes 1671168 | tf_op jit(solution)/shard_map/all_gather | solution.py:159
  19.9 2.0 copy-start.1
  132.6 48.1 %all-to-all-start.1 = ((f32[8,2,1024]{2,1,0:T(2,128)}), f32[8,2,1024]{2,1,0:T(2,128)S(1)}, u32[]{:S(2)}, u32[]{:S(2)}) async-start(f32[8,2,1024]{2,1,0:T(2,128)} %pad_maximum_fusion.1), calls=%async_computation.1 | async-start | bytes 131072 | tf_op jit(solution)/shard_map/all_to_all | solution.py:221
Sparse Core Ops, SparseCore 0:
  37.8 8.0 all-gather.3

commit v4 on v3

--- a/solution.py
+++ b/solution.py
@@ -156,7 +156,10 @@
     mine = lax.dynamic_slice_in_dim(packed, lax.axis_index("rows") * share, share, 0)
     spread = jnp.broadcast_to(mine[None], (ncols, share, own_targets))
     halves = lax.all_to_all(spread, "cols", 0, 0, tiled=True)
-    gathered = lax.all_gather(halves, "rows", axis=1, tiled=True)
+    other = lax.ppermute(halves, "rows", [(0, 1), (1, 0)])
+    first = lax.axis_index("rows") == 0
+    gathered = jnp.concatenate(
+        [jnp.where(first, halves, other), jnp.where(first, other, halves)], axis=1)
     nt = ncols * own_targets
     tblocks = nt // BLK
     blocks = jnp.transpose(
@@ -220,7 +223,9 @@
     parts = jnp.stack([gtop.reshape(ncols, own_targets), gsum.reshape(ncols, own_targets)], axis=1)
     mine = lax.all_to_all(parts, "cols", 0, 0, tiled=True)
     top, total = merge(mine[:, 0, :], mine[:, 1, :], 0)
-    both = lax.all_gather(jnp.concatenate([top, total], axis=0), "rows")
+    here = jnp.concatenate([top, total], axis=0)
+    there = lax.ppermute(here, "rows", [(0, 1), (1, 0)])
+    both = jnp.stack([jnp.where(first, here, there), jnp.where(first, there, here)])
     top, total = merge(both[:, 0, :], both[:, 1, :], 0)
     new_tgt_pot = (-epsilon * LN2) * (top[0] + jnp.log2(total[0]))
     return (src_pot, new_tgt_pot)

time: 201 us -> 178 us (0.89)
  starting transfers between devices: 48.5 us -> 8.98 us
  Pallas kernels: 82.1 us -> 119 us
  between operations: 14.2 us -> 0.79 us
  waiting for transfers between devices: 24.2 us -> 13.9 us
  blocking collectives: 12.2 us -> 18 us
  local copies, waits for them, and re-layouts: 11.7 us -> 9.23 us
    all_to_all x1 -> x0, starting transfers between devices: 41.1 us -> none  [on_device(): mine = lax.all_to_all(parts, 'cols', 0, 0, tiled=True)]
    pallas_call x1, Pallas kernels: 82.1 us -> 119 us  [on_device(): pl.pallas_call(functools.partial(sinkhorn_kernel, npairs, d), grid_spec=g...]
    all_to_all x0 -> x1, blocking collectives: none -> 18 us  [on_device(): mine = lax.all_to_all(parts, 'cols', 0, 0, tiled=True)]
    all_gather x1 -> x0, blocking collectives: 12.2 us -> none  [on_device(): both = lax.all_gather(jnp.concatenate([top, total], axis=0), 'rows')]
    all_gather x1 -> x0, waiting for transfers between devices: 7.32 us -> none  [on_device(): gathered = lax.all_gather(halves, 'rows', axis=1, tiled=True)]
    all_to_all x1 -> x0, waiting for transfers between devices: 4.09 us -> none  [on_device(): mine = lax.all_to_all(parts, 'cols', 0, 0, tiled=True)]
  transfers between devices with their start and end apart: 3 -> 3, of which waited for: 3 -> 2; matrix products, arithmetic and copies ran while one was open for 5% -> 6% of each run, Pallas kernels for 0% -> 0%
where the time goes in v4:
time: 178 us
  Pallas kernels  119 us (67%)
  blocking collectives  18 us (10%)
  waiting for transfers between devices  13.9 us (8%)
  local copies, waits for them, and re-layouts  9.23 us (5%)
  starting transfers between devices  8.98 us (5%)
  other arithmetic  7.58 us (4%)
    pallas_call x1, Pallas kernels, on_device(): pl.pallas_call(functools.partial(sinkhorn_kernel, npairs, d), grid_spec=g...  119 us
    all_to_all x1, blocking collectives, on_device(): mine = lax.all_to_all(parts, 'cols', 0, 0, tiled=True)  18 us
    all_to_all x1, waiting for transfers between devices, on_device(): halves = lax.all_to_all(spread, 'cols', 0, 0, tiled=True)  12.7 us
    all_to_all x1, starting transfers between devices, on_device(): halves = lax.all_to_all(spread, 'cols', 0, 0, tiled=True)  7.28 us
  transfers between devices with their start and end apart: 3, of which 2 were waited for; matrix products, arithmetic and copies ran while one was open for 6% of the time, Pallas kernels for 0%

profile of v4, /device:TPU:0, one launch (start us, length us, event | category | flops | bytes accessed | tf_op | source)
XLA Modules:
  0.0 177.7 jit_solution(1588294095054498814)
XLA Ops:
  0.6 0.0 copy-start.2
  0.6 1.0 fusion.5
  1.6 0.0 copy-start
  1.6 1.0 broadcast_in_dim.31
  2.6 7.3 %all-to-all-start = ((f32[8,17,1024]{2,1,0:T(8,128)}), f32[8,17,1024]{2,1,0:T(8,128)S(1)}, u32[]{:S(2)}, u32[]{:S(2)}) async-start(f32[8,17,1024]{2,1,0:T(8,128)} %broadcast_in_dim.31), calls=%async_computation | async-start | bytes 1572864 | tf_op jit(solution)/shard_map/all_to_all | solution.py:158
  9.9 0.0 copy-done.2
  9.9 0.7 reshape.274.pairs_ref
  10.6 0.6 convert_element_type.27.sel_ref
  11.3 0.0 copy-done
  11.3 2.0 %copy.33 = f32[32,4096]{0,1:T(8,128)} copy(f32[32,4096]{1,0:T(8,128)S(1)} %copy-done) | data formatting | bytes 1048576 | tf_op args[0]
  13.2 0.0 copy-start.1
  13.2 0.1 multiply_reduce_fusion
  13.3 1.9 %copy.37.xn_ref = f32[4096,1]{1,0:T(8,128)} copy(f32[4096,1]{0,1:T(1,128)S(1)} %bitcast.40) | data formatting | bytes 32768 | tf_op jit(solution)/shard_map/broadcast_in_dim | solution.py:185
  15.2 0.0 copy-done.1
  15.2 2.0 %copy.38.ls_ref = f32[4096,1]{1,0:T(8,128)} copy(f32[4096,1]{0,1:T(1,128)S(1)} %bitcast.47) | data formatting | bytes 32768 | tf_op jit(solution)/shard_map/broadcast_in_dim | solution.py:186
  17.2 0.1 fusion.13
  17.3 12.7 %all-to-all-done = f32[8,17,1024]{2,1,0:T(8,128)S(1)} async-done(((f32[8,17,1024]{2,1,0:T(8,128)}), f32[8,17,1024]{2,1,0:T(8,128)S(1)}, u32[]{:S(2)}, u32[]{:S(2)}) %all-to-all-start) | async-done | bytes 557088 | tf_op jit(solution)/shard_map/all_to_all | solution.py:158
  30.0 0.3 copy.34
  30.4 0.1 collective-permute-start
  30.5 0.1 iota_compare_fusion
  30.5 0.1 fusion.12
  30.6 0.6 add_convert_fusion.expand_ref
  31.3 1.1 collective-permute-done
  32.4 0.4 copy_select_fusion.1
  32.8 0.1 fusion.2
  32.9 0.1 fusion
  33.0 1.3 reshape.275.blocks_ref
  34.3 119.3 %shard_map.86 = (f32[4096,1]{1,0:T(8,128)}, f32[32,1,256]{2,1,0:T(1,128)}, f32[32,1,256]{2,1,0:T(1,128)}) custom-call(s32[384]{0:T(512)} %reshape.274.pairs_ref, s32[16]{0:T(128)} %counts_ref.1, f32[4096,32]{1,0:T(8,128)} %bitcast.39, f32[4096,1]{1,0:T(8,128)} %copy.37.xn_ref, f32[4096,1]{1,0:T(8,128)} %copy.38.ls_ref, ...), custom_call_target="tpu_custom_call" | custom-call | tf_op jit(solution)/shard_map/pallas_call | solution.py:210
  153.6 0.8 pad_maximum_fusion.1
  154.4 18.0 %all_to_all.10 = f32[8,2,1024]{2,1,0:T(2,128)S(1)} all-to-all(f32[8,2,1024]{2,1,0:T(2,128)S(1)} %pad_maximum_fusion.1), channel_id=1, replica_groups=mesh['parts'=2,'rows'=2,'cols'=8] {'cols'}, dimensions={0} | all-to-all | bytes 131072 | tf_op jit(solution)/shard_map/all_to_all | solution.py:224
  172.4 0.1 slice_reduce_fusion
  172.5 1.6 collective-permute-start.1
  174.2 2.8 %reduce.2 = f32[4096]{0:T(1024)} reduce(f32[4096,1]{1,0:T(8,128)} %get-tuple-element.5, f32[]{:T(128)} %constant.48), dimensions={1}, to_apply=%get-tuple-element.5.reduce_sub_computation | reduce | bytes 32772 | tf_op jit(solution)/shard_map/pallas_call | solution.py:210
  177.0 0.0 collective-permute-done.1
  177.1 0.6 add_multiply_fusion
  (15 shorter events, 0.2 us)
Async XLA Ops:
  0.6 9.3 %copy-start.2 = (s32[16,24]{1,0:T(8,128)S(1)}, s32[16,24]{1,0:T(8,128)}, u32[]{:S(2)}) copy-start(s32[16,24]{1,0:T(8,128)} %param.12) | copy-start | bytes 4612
  1.6 9.6 %copy-start = (f32[32,4096]{1,0:T(8,128)S(1)}, f32[32,4096]{1,0:T(8,128)}, u32[]{:S(2)}) copy-start(f32[32,4096]{1,0:T(8,128)} %param.7) | copy-start | bytes 1572868
  2.6 27.4 %all-to-all-start = ((f32[8,17,1024]{2,1,0:T(8,128)}), f32[8,17,1024]{2,1,0:T(8,128)S(1)}, u32[]{:S(2)}, u32[]{:S(2)}) async-start(f32[8,17,1024]{2,1,0:T(8,128)} %broadcast_in_dim.31), calls=%async_computation | async-start | bytes 1572864 | tf_op jit(solution)/shard_map/all_to_all | solution.py:158
  13.2 2.0 %copy-start.1 = (f32[4096]{0:T(1024)S(1)}, f32[4096]{0:T(1024)}, u32[]{:S(2)}) copy-start(f32[4096]{0:T(1024)} %param.10) | copy-start | bytes 49156
  30.4 2.0 %collective-permute-start = (f32[8,17,1024]{2,0,1:T(8,128)S(1)}, f32[8,17,1024]{2,0,1:T(8,128)S(1)}, u32[]{:S(2)}, u32[]{:S(2)}) collective-permute-start(f32[8,17,1024]{2,0,1:T(8,128)S(1)} %copy.34), channel_id=1, source_target_pairs={{0,8},{8,0},{1,9},{9,1},{2,10},{10,2},{3,11},{11,3},{4,12},{12,4},... | collective-permute-start | bytes 1671176 | tf_op jit(solution)/shard_map/ppermute | solution.py:159
  172.5 4.4 %collective-permute-start.1 = (f32[2,1024]{1,0:T(2,128)S(1)}, f32[2,1024]{1,0:T(2,128)S(1)}, u32[]{:S(2)}, u32[]{:S(2)}) collective-permute-start(f32[2,1024]{1,0:T(2,128)S(1)} %pad_maximum_fusion.3), channel_id=1, source_target_pairs={{0,8},{8,0},{1,9},{9,1},{2,10},{10,2},{3,11},{11,3},{4,12},{12,4},... | collective-permute-start | bytes 24584 | tf_op jit(solution)/shard_map/ppermute | solution.py:227

commit v5 on v4

--- a/solution.py
+++ b/solution.py
@@ -94,6 +94,22 @@
         def _last():
             body([cnt - 1])
 
+    def quads_of(body):
+        def four(k, carry):
+            body([4 * k + i for i in range(4)])
+            return carry
+
+        lax.fori_loop(0, cnt // 4, four, 0)
+        done = cnt - cnt % 4
+
+        @pl.when(cnt % 4 >= 2)
+        def _pair():
+            body([done, done + 1])
+
+        @pl.when(cnt % 2 == 1)
+        def _last():
+            body([cnt - 1])
+
     def row_pass(ts):
         halves = []
         for t in ts:
@@ -132,7 +148,7 @@
             gsum_ref[tb] = gsum_ref[tb] * jnp.exp2(old - new) + cs * jnp.exp2(cm - new)
             gtop_ref[tb] = new
 
-    pairs_of(col_pass)
+    quads_of(col_pass)
 
 
 def merge(tops, sums, axis):
@@ -201,7 +217,7 @@
             pl.BlockSpec((tblocks, 1, BLK), lambda b, pr, ct: (0, 0, 0)),
             pl.BlockSpec((tblocks, 1, BLK), lambda b, pr, ct: (0, 0, 0)),
         ],
-        scratch_shapes=[pltpu.VMEM((2, BLK, BLK), jnp.float32),
+        scratch_shapes=[pltpu.VMEM((4, BLK, BLK), jnp.float32),
                         pltpu.VMEM((BLK, KP), jnp.bfloat16),
                         pltpu.VMEM((BLK, KP), jnp.bfloat16),
                         pltpu.VMEM((2, BLK, LANE), jnp.float32),

time: 178 us -> 156 us (0.88)
  Pallas kernels: 119 us -> 94.2 us
  blocking collectives: 18 us -> 22.3 us
    pallas_call x1, Pallas kernels: 119 us -> 94.2 us  [on_device(): pl.pallas_call(functools.partial(sinkhorn_kernel, npairs, d), grid_spec=g...]
    all_to_all x1, blocking collectives: 18 us -> 22.3 us  [on_device(): mine = lax.all_to_all(parts, 'cols', 0, 0, tiled=True)]
  transfers between devices with their start and end apart: 3 -> 3, of which waited for: 2 -> 2; matrix products, arithmetic and copies ran while one was open for 6% -> 7% of each run, Pallas kernels for 0% -> 0%
where the time goes in v5:
time: 156 us
  Pallas kernels  94.2 us (60%)
  blocking collectives  22.3 us (14%)
  waiting for transfers between devices  13.9 us (9%)
  local copies, waits for them, and re-layouts  9.23 us (6%)
  other arithmetic  7.58 us (5%)
  starting transfers between devices  7.55 us (5%)
    pallas_call x1, Pallas kernels, on_device(): pl.pallas_call(functools.partial(sinkhorn_kernel, npairs, d), grid_spec=g...  94.2 us
    all_to_all x1, blocking collectives, on_device(): mine = lax.all_to_all(parts, 'cols', 0, 0, tiled=True)  22.3 us
    all_to_all x1, waiting for transfers between devices, on_device(): halves = lax.all_to_all(spread, 'cols', 0, 0, tiled=True)  12.7 us
    all_to_all x1, starting transfers between devices, on_device(): halves = lax.all_to_all(spread, 'cols', 0, 0, tiled=True)  7.28 us
  transfers between devices with their start and end apart: 3, of which 2 were waited for; matrix products, arithmetic and copies ran while one was open for 7% of the time, Pallas kernels for 0%

profile of v5, /device:TPU:0, one launch (start us, length us, event | category | flops | bytes accessed | tf_op | source)
XLA Modules:
  0.0 155.6 jit_solution(7608156628644828565)
XLA Ops:
  0.6 0.0 copy-start.2
  0.6 1.0 fusion.5
  1.6 0.0 copy-start
  1.6 1.0 broadcast_in_dim.31
  2.6 7.3 %all-to-all-start = ((f32[8,17,1024]{2,1,0:T(8,128)}), f32[8,17,1024]{2,1,0:T(8,128)S(1)}, u32[]{:S(2)}, u32[]{:S(2)}) async-start(f32[8,17,1024]{2,1,0:T(8,128)} %broadcast_in_dim.31), calls=%async_computation | async-start | bytes 1572864 | tf_op jit(solution)/shard_map/all_to_all | solution.py:174
  9.9 0.0 copy-done.2
  9.9 0.7 reshape.274.pairs_ref
  10.6 0.6 convert_element_type.27.sel_ref
  11.3 0.0 copy-done
  11.3 2.0 %copy.33 = f32[32,4096]{0,1:T(8,128)} copy(f32[32,4096]{1,0:T(8,128)S(1)} %copy-done) | data formatting | bytes 1048576 | tf_op args[0]
  13.2 0.0 copy-start.1
  13.2 0.1 multiply_reduce_fusion
  13.3 1.9 %copy.37.xn_ref = f32[4096,1]{1,0:T(8,128)} copy(f32[4096,1]{0,1:T(1,128)S(1)} %bitcast.40) | data formatting | bytes 32768 | tf_op jit(solution)/shard_map/broadcast_in_dim | solution.py:201
  15.2 0.0 copy-done.1
  15.2 2.0 %copy.38.ls_ref = f32[4096,1]{1,0:T(8,128)} copy(f32[4096,1]{0,1:T(1,128)S(1)} %bitcast.47) | data formatting | bytes 32768 | tf_op jit(solution)/shard_map/broadcast_in_dim | solution.py:202
  17.2 0.1 fusion.13
  17.3 12.7 %all-to-all-done = f32[8,17,1024]{2,1,0:T(8,128)S(1)} async-done(((f32[8,17,1024]{2,1,0:T(8,128)}), f32[8,17,1024]{2,1,0:T(8,128)S(1)}, u32[]{:S(2)}, u32[]{:S(2)}) %all-to-all-start) | async-done | bytes 557088 | tf_op jit(solution)/shard_map/all_to_all | solution.py:174
  30.0 0.3 copy.34
  30.4 0.1 collective-permute-start
  30.5 0.1 iota_compare_fusion
  30.5 0.1 fusion.12
  30.6 0.6 add_convert_fusion.expand_ref
  31.3 1.1 collective-permute-done
  32.4 0.4 copy_select_fusion.1
  32.8 0.1 fusion.2
  32.9 0.1 fusion
  33.0 1.3 reshape.275.blocks_ref
  34.3 94.2 %shard_map.86 = (f32[4096,1]{1,0:T(8,128)}, f32[32,1,256]{2,1,0:T(1,128)}, f32[32,1,256]{2,1,0:T(1,128)}) custom-call(s32[384]{0:T(512)} %reshape.274.pairs_ref, s32[16]{0:T(128)} %counts_ref.1, f32[4096,32]{1,0:T(8,128)} %bitcast.39, f32[4096,1]{1,0:T(8,128)} %copy.37.xn_ref, f32[4096,1]{1,0:T(8,128)} %copy.38.ls_ref, ...), custom_call_target="tpu_custom_call" | custom-call | tf_op jit(solution)/shard_map/pallas_call | solution.py:226
  128.6 0.8 pad_maximum_fusion.1
  129.4 22.3 %all_to_all.10 = f32[8,2,1024]{2,1,0:T(2,128)S(1)} all-to-all(f32[8,2,1024]{2,1,0:T(2,128)S(1)} %pad_maximum_fusion.1), channel_id=1, replica_groups=mesh['parts'=2,'rows'=2,'cols'=8] {'cols'}, dimensions={0} | all-to-all | bytes 131072 | tf_op jit(solution)/shard_map/all_to_all | solution.py:240
  151.7 0.1 slice_reduce_fusion
  151.8 0.2 collective-permute-start.1
  152.0 2.8 %reduce.2 = f32[4096]{0:T(1024)} reduce(f32[4096,1]{1,0:T(8,128)} %get-tuple-element.5, f32[]{:T(128)} %constant.48), dimensions={1}, to_apply=%get-tuple-element.5.reduce_sub_computation | reduce | bytes 32772 | tf_op jit(solution)/shard_map/pallas_call | solution.py:226
  154.8 0.0 collective-permute-done.1
  155.0 0.6 add_multiply_fusion
  (15 shorter events, 0.2 us)
Async XLA Ops:
  0.6 9.3 %copy-start.2 = (s32[16,24]{1,0:T(8,128)S(1)}, s32[16,24]{1,0:T(8,128)}, u32[]{:S(2)}) copy-start(s32[16,24]{1,0:T(8,128)} %param.12) | copy-start | bytes 4612
  1.6 9.6 %copy-start = (f32[32,4096]{1,0:T(8,128)S(1)}, f32[32,4096]{1,0:T(8,128)}, u32[]{:S(2)}) copy-start(f32[32,4096]{1,0:T(8,128)} %param.7) | copy-start | bytes 1572868
  2.6 27.4 %all-to-all-start = ((f32[8,17,1024]{2,1,0:T(8,128)}), f32[8,17,1024]{2,1,0:T(8,128)S(1)}, u32[]{:S(2)}, u32[]{:S(2)}) async-start(f32[8,17,1024]{2,1,0:T(8,128)} %broadcast_in_dim.31), calls=%async_computation | async-start | bytes 1572864 | tf_op jit(solution)/shard_map/all_to_all | solution.py:174
  13.2 2.0 %copy-start.1 = (f32[4096]{0:T(1024)S(1)}, f32[4096]{0:T(1024)}, u32[]{:S(2)}) copy-start(f32[4096]{0:T(1024)} %param.10) | copy-start | bytes 49156
  30.4 2.0 %collective-permute-start = (f32[8,17,1024]{2,0,1:T(8,128)S(1)}, f32[8,17,1024]{2,0,1:T(8,128)S(1)}, u32[]{:S(2)}, u32[]{:S(2)}) collective-permute-start(f32[8,17,1024]{2,0,1:T(8,128)S(1)} %copy.34), channel_id=1, source_target_pairs={{0,8},{8,0},{1,9},{9,1},{2,10},{10,2},{3,11},{11,3},{4,12},{12,4},... | collective-permute-start | bytes 1671176 | tf_op jit(solution)/shard_map/ppermute | solution.py:175
  151.8 3.0 %collective-permute-start.1 = (f32[2,1024]{1,0:T(2,128)S(1)}, f32[2,1024]{1,0:T(2,128)S(1)}, u32[]{:S(2)}, u32[]{:S(2)}) collective-permute-start(f32[2,1024]{1,0:T(2,128)S(1)} %pad_maximum_fusion.3), channel_id=1, source_target_pairs={{0,8},{8,0},{1,9},{9,1},{2,10},{10,2},{3,11},{11,3},{4,12},{12,4},... | collective-permute-start | bytes 24584 | tf_op jit(solution)/shard_map/ppermute | solution.py:243

commit v6 on v5

--- a/solution.py
+++ b/solution.py
@@ -8,7 +8,7 @@
 from jax.sharding import PartitionSpec as P
 
 BLK = 256
-KP = 256
+KP = 128
 LANE = 128
 
 epsilon = 0.1
@@ -37,7 +37,7 @@
 def build_table(d, blocks_ref, tab_ref):
     scale = 2.0 * LOG2E / epsilon
     slot_row = lax.broadcasted_iota(jnp.int32, (16, BLK), 0)
-    used = 6 * d + 16
+    used = 3 * d + 16
 
     def one(tb, carry):
         blk = blocks_ref[tb]
@@ -48,14 +48,14 @@
         acol = (lt + (tp - yn) / epsilon) * LOG2E
         ccol = (-yn / epsilon) * LOG2E
         y1, y2, y3 = split3_kernel(y * scale)
-        for k, piece in enumerate([y1, y2, y1, y3, y2, y1]):
+        for k, piece in enumerate([y1, y2, y1]):
             tab_ref[tb, k * d:(k + 1) * d, :] = piece
         slot = jnp.zeros((16, BLK), jnp.float32)
         pieces = list(split3_kernel(acol)) + list(split3_kernel(ccol))
         for k, piece in enumerate(pieces):
             slot = jnp.where(slot_row == k, piece.astype(jnp.float32), slot)
         slot = jnp.where((slot_row >= 6) & (slot_row < 9), 1.0, slot)
-        tab_ref[tb, 6 * d:used, :] = slot.astype(jnp.bfloat16)
+        tab_ref[tb, 3 * d:used, :] = slot.astype(jnp.bfloat16)
         tab_ref[tb, used:KP, :] = jnp.zeros((KP - used, BLK), jnp.bfloat16)
         return carry
 
@@ -188,8 +188,8 @@
         for s in starts:
             hit = hit | (col == comp + s)
         return hit.astype(jnp.bfloat16)
-    expand = jnp.stack([place([0, d, 3 * d]), place([2 * d, 4 * d]), place([5 * d])])
-    k0 = 6 * d
+    expand = jnp.stack([place([0, d]), place([2 * d]), place([])])
+    k0 = 3 * d
     sel = jnp.stack([
         ((col[0] >= k0) & (col[0] < k0 + 3)),
         ((col[0] >= k0 + 3) & (col[0] < k0 + 6)),

time: 156 us -> 149 us (0.955)
  Pallas kernels: 94.2 us -> 71.6 us
  blocking collectives: 22.3 us -> 38.9 us
    pallas_call x1, Pallas kernels: 94.2 us -> 71.6 us  [on_device(): pl.pallas_call(functools.partial(sinkhorn_kernel, npairs, d), grid_spec=g...]
    all_to_all x1, blocking collectives: 22.3 us -> 38.9 us  [on_device(): mine = lax.all_to_all(parts, 'cols', 0, 0, tiled=True)]
where the time goes in v6:
time: 149 us; the launch traced here: 150 us
  Pallas kernels  71.6 us (48%)
  blocking collectives  38.9 us (26%)
  waiting for transfers between devices  13.9 us (9%)
  local copies, waits for them, and re-layouts  9.3 us (6%)
  other arithmetic  7.51 us (5%)
  starting transfers between devices  7.42 us (5%)
    pallas_call x1, Pallas kernels, on_device(): pl.pallas_call(functools.partial(sinkhorn_kernel, npairs, d), grid_spec=g...  71.6 us
    all_to_all x1, blocking collectives, on_device(): mine = lax.all_to_all(parts, 'cols', 0, 0, tiled=True)  38.9 us
    all_to_all x1, waiting for transfers between devices, on_device(): halves = lax.all_to_all(spread, 'cols', 0, 0, tiled=True)  12.8 us
    all_to_all x1, starting transfers between devices, on_device(): halves = lax.all_to_all(spread, 'cols', 0, 0, tiled=True)  7.28 us
  transfers between devices with their start and end apart: 3, of which 2 were waited for; matrix products, arithmetic and copies ran while one was open for 7% of the time, Pallas kernels for 0%

profile of v6, /device:TPU:0, one launch (start us, length us, event | category | flops | bytes accessed | tf_op | source)
XLA Modules:
  0.0 149.5 jit_solution(142275206520874415)
XLA Ops:
  0.6 0.0 copy-start.2
  0.6 0.0 copy-start
  0.7 1.0 fusion.5
  1.7 1.0 broadcast_in_dim.31
  2.7 7.3 %all-to-all-start = ((f32[8,17,1024]{2,1,0:T(8,128)}), f32[8,17,1024]{2,1,0:T(8,128)S(1)}, u32[]{:S(2)}, u32[]{:S(2)}) async-start(f32[8,17,1024]{2,1,0:T(8,128)} %broadcast_in_dim.31), calls=%async_computation | async-start | bytes 1572864 | tf_op jit(solution)/shard_map/all_to_all | solution.py:174
  9.9 0.0 copy-done.2
  10.0 0.7 reshape.163.pairs_ref
  10.7 0.6 convert_element_type.25.sel_ref
  11.3 0.0 copy-done
  11.3 2.0 %copy.33 = f32[32,4096]{0,1:T(8,128)} copy(f32[32,4096]{1,0:T(8,128)S(1)} %copy-done) | data formatting | bytes 1048576 | tf_op args[0]
  13.3 0.0 copy-start.1
  13.3 0.1 multiply_reduce_fusion
  13.3 1.9 %copy.37.xn_ref = f32[4096,1]{1,0:T(8,128)} copy(f32[4096,1]{0,1:T(1,128)S(1)} %bitcast.41) | data formatting | bytes 32768 | tf_op jit(solution)/shard_map/broadcast_in_dim | solution.py:201
  15.3 0.0 copy-done.1
  15.3 2.0 %copy.38.ls_ref = f32[4096,1]{1,0:T(8,128)} copy(f32[4096,1]{0,1:T(1,128)S(1)} %bitcast.48) | data formatting | bytes 32768 | tf_op jit(solution)/shard_map/broadcast_in_dim | solution.py:202
  17.3 0.1 pad.17.clone
  17.3 12.8 %all-to-all-done = f32[8,17,1024]{2,1,0:T(8,128)S(1)} async-done(((f32[8,17,1024]{2,1,0:T(8,128)}), f32[8,17,1024]{2,1,0:T(8,128)S(1)}, u32[]{:S(2)}, u32[]{:S(2)}) %all-to-all-start) | async-done | bytes 557088 | tf_op jit(solution)/shard_map/all_to_all | solution.py:174
  30.1 0.3 copy.34
  30.4 0.1 collective-permute-start
  30.5 0.1 fusion.12
  30.6 0.7 maximum_maximum_fusion.expand_ref
  31.3 1.2 collective-permute-done
  32.5 0.4 copy_select_fusion.1
  32.8 0.1 fusion.2
  32.9 0.1 fusion
  33.1 1.3 reshape.164.blocks_ref
  34.4 71.6 %shard_map.86 = (f32[4096,1]{1,0:T(8,128)}, f32[32,1,256]{2,1,0:T(1,128)}, f32[32,1,256]{2,1,0:T(1,128)}) custom-call(s32[384]{0:T(512)} %reshape.163.pairs_ref, s32[16]{0:T(128)} %counts_ref.1, f32[4096,32]{1,0:T(8,128)} %bitcast.40, f32[4096,1]{1,0:T(8,128)} %copy.37.xn_ref, f32[4096,1]{1,0:T(8,128)} %copy.38.ls_ref, ...), custom_call_target="tpu_custom_call" | custom-call | tf_op jit(solution)/shard_map/pallas_call | solution.py:226
  106.0 0.8 pad_maximum_fusion.1
  106.8 38.9 %all_to_all.10 = f32[8,2,1024]{2,1,0:T(2,128)S(1)} all-to-all(f32[8,2,1024]{2,1,0:T(2,128)S(1)} %pad_maximum_fusion.1), channel_id=1, replica_groups=mesh['parts'=2,'rows'=2,'cols'=8] {'cols'}, dimensions={0} | all-to-all | bytes 131072 | tf_op jit(solution)/shard_map/all_to_all | solution.py:240
  145.8 0.1 slice_reduce_fusion
  145.9 0.1 collective-permute-start.1
  146.0 2.8 %reduce.2 = f32[4096]{0:T(1024)} reduce(f32[4096,1]{1,0:T(8,128)} %get-tuple-element.5, f32[]{:T(128)} %constant.44), dimensions={1}, to_apply=%get-tuple-element.5.reduce_sub_computation | reduce | bytes 32772 | tf_op jit(solution)/shard_map/pallas_call | solution.py:226
  148.8 0.0 collective-permute-done.1
  148.9 0.6 add_multiply_fusion
  (14 shorter events, 0.2 us)
Async XLA Ops:
  0.6 9.3 %copy-start.2 = (s32[16,24]{1,0:T(8,128)S(1)}, s32[16,24]{1,0:T(8,128)}, u32[]{:S(2)}) copy-start(s32[16,24]{1,0:T(8,128)} %param.12) | copy-start | bytes 4612
  0.6 10.6 %copy-start = (f32[32,4096]{1,0:T(8,128)S(1)}, f32[32,4096]{1,0:T(8,128)}, u32[]{:S(2)}) copy-start(f32[32,4096]{1,0:T(8,128)} %param.7) | copy-start | bytes 1572868
  2.7 27.4 %all-to-all-start = ((f32[8,17,1024]{2,1,0:T(8,128)}), f32[8,17,1024]{2,1,0:T(8,128)S(1)}, u32[]{:S(2)}, u32[]{:S(2)}) async-start(f32[8,17,1024]{2,1,0:T(8,128)} %broadcast_in_dim.31), calls=%async_computation | async-start | bytes 1572864 | tf_op jit(solution)/shard_map/all_to_all | solution.py:174
  13.3 2.0 %copy-start.1 = (f32[4096]{0:T(1024)S(1)}, f32[4096]{0:T(1024)}, u32[]{:S(2)}) copy-start(f32[4096]{0:T(1024)} %param.10) | copy-start | bytes 49156
  30.4 2.0 %collective-permute-start = (f32[8,17,1024]{2,0,1:T(8,128)S(1)}, f32[8,17,1024]{2,0,1:T(8,128)S(1)}, u32[]{:S(2)}, u32[]{:S(2)}) collective-permute-start(f32[8,17,1024]{2,0,1:T(8,128)S(1)} %copy.34), channel_id=1, source_target_pairs={{0,8},{8,0},{1,9},{9,1},{2,10},{10,2},{3,11},{11,3},{4,12},{12,4},... | collective-permute-start | bytes 1671176 | tf_op jit(solution)/shard_map/ppermute | solution.py:175
  145.9 2.9 %collective-permute-start.1 = (f32[2,1024]{1,0:T(2,128)S(1)}, f32[2,1024]{1,0:T(2,128)S(1)}, u32[]{:S(2)}, u32[]{:S(2)}) collective-permute-start(f32[2,1024]{1,0:T(2,128)S(1)} %pad_maximum_fusion.3), channel_id=1, source_target_pairs={{0,8},{8,0},{1,9},{9,1},{2,10},{10,2},{3,11},{11,3},{4,12},{12,4},... | collective-permute-start | bytes 24584 | tf_op jit(solution)/shard_map/ppermute | solution.py:243
